TPU v7x, 256 devices: a whole 4x4x8 slice. The times are simulated.
256 devices in a mesh: row: 32 (over x_hi, z, core), col: 8 (over y, x_lo).
Axes of the slice: x: 4 (x_hi: 2, x_lo: 2; x = x_hi * 2 + x_lo), y: 4, z: 8, core: 2. Of those that a mesh axis runs over, the one named last changes fastest.
Arguments:
- features: bfloat16 [8, 32, 128, 512], P('col', 'row'), may hold values from -6 to 6
- weight: bfloat16 [512, 512], replicated, may hold values from -0.25 to 0.25
- cotangent: bfloat16 [32, 8, 128, 512], P('row', 'col'), may hold values from -6 to 6
- tile_vals: bfloat16 [32, 8, 128, 128, 128], P('row', 'col'), may hold values from 0 to 1
- tile_rows: int32 [32, 8, 128], P('row', 'col'), may hold values from 0 to 7, as said below
- tile_cols: int32 [32, 8, 128], P('row', 'col'), may hold values from 0 to 31
- tile_count: int32 [32, 8], P('row', 'col'), may hold values from 32 to 128, as said below
Outputs:
- layer_out: bfloat16 [32, 8, 128, 512], P('row', 'col')
- weight_grad: float32 [512, 512], replicated
- feature_grad: bfloat16 [8, 32, 128, 512], P('col', 'row')
Inputs may be any that keep to these rules, and one draw needn't show every extreme that they name: `tile_count`: live tile slots of each grid block; in every draw one block, drawn from the seed, has all 128 live. The (tile_rows, tile_cols) pairs of the 128 slots of one grid block are distinct.
All inputs are finite; a program needn't handle non-finite values.
Results may differ from a plain program's by a relative error of at most 0.005.
Values may be sent and summed in bfloat16 or wider, within the bound.
No kernel may reach another device: no remote copies, remote signals or barrier semaphores. Data moves between devices by JAX's collectives and lax.ppermute only.
A program may use at most 128 MiB of HBM per device.

v0:
```python
import math

import jax
import jax.numpy as jnp
from jax import lax
from jax.sharding import PartitionSpec as P


def per_device(features, weight, cotangent, tile_vals, tile_rows, tile_cols, tile_count):
    sub_rows = features.shape[2]
    width = features.shape[3]
    slots = tile_vals.shape[2]
    tile = tile_vals.shape[3]
    rows_axis = lax.axis_size("row")
    cols_axis = lax.axis_size("col")
    tile_rows_blk = sub_rows * cols_axis // tile
    tile_cols_blk = sub_rows * rows_axis // tile
    group = math.gcd(slots, 16)
    turns = slots // group
    live = jnp.arange(slots, dtype=jnp.int32) < tile_count[0, 0]
    masked = jnp.where(live[:, None, None], tile_vals[0, 0], jnp.zeros((), jnp.bfloat16))
    blocks = masked.reshape(turns, group, tile, tile)
    row_groups = tile_rows[0, 0].reshape(turns, group)
    col_groups = tile_cols[0, 0].reshape(turns, group)
    panel = lax.all_gather(features, "row", axis=1, tiled=True).reshape(tile_cols_blk, tile, width)

    def forward_step(carry, items):
        total, degsum = carry
        block, rid, cid = items
        prod = jnp.einsum("gij,gjf->gif", block, panel[cid], preferred_element_type=jnp.float32)
        total = total.at[rid].add(prod)
        degsum = degsum.at[rid].add(jnp.sum(block, axis=2, dtype=jnp.float32))
        return ((total, degsum), None)

    init = (
        jnp.zeros((tile_rows_blk, tile, width), jnp.float32),
        jnp.zeros((tile_rows_blk, tile), jnp.float32),
    )
    (total, degsum), _ = lax.scan(forward_step, init, (blocks, row_groups, col_groups))
    partial_agg = total.reshape(tile_rows_blk * tile, width)
    local_deg = degsum.reshape(tile_rows_blk * tile)
    summed, deg_own = (
        lax.psum_scatter(partial_agg, "col", scatter_dimension=0, tiled=True),
        lax.psum_scatter(local_deg, "col", scatter_dimension=0, tiled=True),
    )
    inv_own = lax.rsqrt(1.0 + deg_own)
    aggregated = (inv_own[:, None] * summed).astype(jnp.bfloat16)
    layer_out = jnp.dot(aggregated, weight, preferred_element_type=jnp.float32).astype(jnp.bfloat16)
    grad_own = cotangent[0, 0]
    nodes = sub_rows * rows_axis * cols_axis
    weight_term = lax.dot_general(
        aggregated, grad_own, (((0,), (0,)), ((), ())), preferred_element_type=jnp.float32
    )
    weight_grad = lax.psum(weight_term, ("row", "col")) * nodes ** (-0.5)
    projected = lax.dot_general(
        grad_own, weight, (((1,), (1,)), ((), ())), preferred_element_type=jnp.float32
    )
    scaled_own = (inv_own[:, None] * projected).astype(jnp.bfloat16)
    scaled = lax.all_gather(scaled_own, "col", axis=0, tiled=True)
    scaled_tiles = scaled.reshape(tile_rows_blk, tile, width)

    def backward_step(back, items):
        block, rid, cid = items
        prod = jnp.einsum(
            "gji,gjf->gif", block, scaled_tiles[rid], preferred_element_type=jnp.float32
        )
        return (back.at[cid].add(prod), None)

    back, _ = lax.scan(
        backward_step,
        jnp.zeros((tile_cols_blk, tile, width), jnp.float32),
        (blocks, row_groups, col_groups),
    )
    grad_term = back.reshape(tile_cols_blk * tile, width)
    feature_grad = lax.psum_scatter(grad_term, "row", scatter_dimension=0, tiled=True).astype(
        jnp.bfloat16
    )
    return (
        layer_out.reshape(1, 1, sub_rows, width),
        weight_grad,
        feature_grad.reshape(1, 1, sub_rows, width),
    )


def solution(mesh):
    return jax.shard_map(
        per_device,
        mesh=mesh,
        in_specs=(
            P("col", "row", None, None),
            P(),
            P("row", "col", None, None),
            P("row", "col", None, None, None),
            P("row", "col", None),
            P("row", "col", None),
            P("row", "col"),
        ),
        out_specs=(P("row", "col", None, None), P(), P("col", "row", None, None)),
        check_vma=False,
    )
```

profile of v0, /device:TPU:2, one launch (start us, length us, event | category | flops | bytes accessed | tf_op | source)
XLA Modules:
  0.0 777.5 jit_solution(3033897492894014110)
XLA Ops:
  11.9 6.4 copy.12
  22.8 76.6 %all-gather.3.cloned.1.call-done = bf16[1,32,128,512]{3,2,0,1:T(8,128)(2,1)} async-done(((bf16[1,1,128,512]{3,2,0,1:T(8,128)(2,1)}), bf16[1,32,128,512]{3,2,0,1:T(8,128)(2,1)}) %all-gather.3.cloned.1.call-update) | async-done | bytes 4194320 | tf_op jit(solution)/shard_map/all_gather | solution.py:25
  99.7 150.0 %while.22 = (s32[]{:T(128)}, f32[8,128,512]{2,1,0:T(8,128)S(1)}, f32[8,128]{1,0:T(8,128)S(1)}, s32[8,16]{1,0:T(8,128)S(1)}, bf16[8,16,128,128]{2,3,1,0:T(8,128)(...) while((s32[]{:T(128)}, f32[8,128,512]{2,1,0:T(8,128)S(1)}, ...), condition=%wide.region_4.5_spmd, body=%wide.region_0.4_spmd.sunk | while | flops 270009440 | bytes 26251876 | solution.py:39
  112.3 6.2 scatter_fusion
  131.1 6.2 scatter_fusion
  168.5 6.2 scatter_fusion
  187.3 6.2 scatter_fusion
  206.0 6.2 scatter_fusion
  224.8 6.1 scatter_fusion
  243.5 6.1 scatter_fusion
  252.4 17.8 %all-reduce = f32[1024]{0:T(1024)S(1)} all-reduce(f32[1024]{0:T(1024)S(1)} %bitcast.84), channel_id=2, replica_groups=mesh['row'=32,'col'=8] {'col'}, use_global_device_ids=true, to_apply=%region_5.6.clone | all-reduce | flops 1024 | bytes 8192
  271.3 31.2 %reduce-scatter.3.cloned.1.call-done = f32[128,512]{1,0:T(8,128)} async-done(((f32[1024,512]{1,0:T(8,128)}), f32[128,512]{1,0:T(8,128)}) %reduce-scatter.3.cloned.1.call-update) | async-done | bytes 262160 | tf_op jit(solution)/shard_map/reduce_scatter | solution.py:43
  304.9 41.5 %all-gather.5.cloned.1.call-done = bf16[1024,512]{1,0:T(8,128)(2,1)} async-done(((bf16[128,512]{1,0:T(8,128)(2,1)}), bf16[1024,512]{1,0:T(8,128)(2,1)}) %all-gather.5.cloned.1.call-update) | async-done | bytes 1048592 | tf_op jit(solution)/shard_map/all_gather | solution.py:59
  350.7 121.8 %while.23 = (s32[]{:T(128)}, f32[32,128,512]{2,1,0:T(8,128)}, s32[8,16]{1,0:T(8,128)S(1)}, bf16[8,16,128,128]{2,3,1,0:T(8,128)(2,1)}, s32[8,16]{1,0:T(8,128)S(1)}, /*index=5*/bf16[8,128,512]{2,1,0:T(8,128)(2,1)}, s32[]{:T(128)}) while((s32[]{:T(128)}, f32[32,128,512]{2,1,0:T(8,128)}, s32[8,16]{1,0:T(8,128)S(1)}, ...), condition=%wide.region_10.11_spmd, body=%wide.region_8.10_spmd.sunk | while | flops 269485152 | bytes 23597596 | solution.py:69
  356.3 9.5 %scatter_fusion.2 = f32[32,128,512]{2,1,0:T(8,128)} fusion(f32[32,128,512]{2,1,0:T(8,128)} %get-tuple-element.240, s32[16]{0:T(128)S(1)} %get-tuple-element.206, f32[16,128,512]{2,1,0:T(8,128)} %fusion.39), kind=kCustom, calls=%fused_computation.4.clone.1 | custom fusion | flops 1048576 | bytes 12582976 | tf_op jit(solution)/shard_map/while/body/eval_jaxpr/scatter-add | solution.py:67
  371.5 9.7 %scatter_fusion.2 = f32[32,128,512]{2,1,0:T(8,128)} fusion(f32[32,128,512]{2,1,0:T(8,128)} %get-tuple-element.240, s32[16]{0:T(128)S(1)} %get-tuple-element.206, f32[16,128,512]{2,1,0:T(8,128)} %fusion.39), kind=kCustom, calls=%fused_computation.4.clone.1 | custom fusion | flops 1048576 | bytes 12582976 | tf_op jit(solution)/shard_map/while/body/eval_jaxpr/scatter-add | solution.py:67
  386.8 9.6 %scatter_fusion.2 = f32[32,128,512]{2,1,0:T(8,128)} fusion(f32[32,128,512]{2,1,0:T(8,128)} %get-tuple-element.240, s32[16]{0:T(128)S(1)} %get-tuple-element.206, f32[16,128,512]{2,1,0:T(8,128)} %fusion.39), kind=kCustom, calls=%fused_computation.4.clone.1 | custom fusion | flops 1048576 | bytes 12582976 | tf_op jit(solution)/shard_map/while/body/eval_jaxpr/scatter-add | solution.py:67
  402.1 9.5 %scatter_fusion.2 = f32[32,128,512]{2,1,0:T(8,128)} fusion(f32[32,128,512]{2,1,0:T(8,128)} %get-tuple-element.240, s32[16]{0:T(128)S(1)} %get-tuple-element.206, f32[16,128,512]{2,1,0:T(8,128)} %fusion.39), kind=kCustom, calls=%fused_computation.4.clone.1 | custom fusion | flops 1048576 | bytes 12582976 | tf_op jit(solution)/shard_map/while/body/eval_jaxpr/scatter-add | solution.py:67
  417.2 9.5 %scatter_fusion.2 = f32[32,128,512]{2,1,0:T(8,128)} fusion(f32[32,128,512]{2,1,0:T(8,128)} %get-tuple-element.240, s32[16]{0:T(128)S(1)} %get-tuple-element.206, f32[16,128,512]{2,1,0:T(8,128)} %fusion.39), kind=kCustom, calls=%fused_computation.4.clone.1 | custom fusion | flops 1048576 | bytes 12582976 | tf_op jit(solution)/shard_map/while/body/eval_jaxpr/scatter-add | solution.py:67
  432.4 9.6 %scatter_fusion.2 = f32[32,128,512]{2,1,0:T(8,128)} fusion(f32[32,128,512]{2,1,0:T(8,128)} %get-tuple-element.240, s32[16]{0:T(128)S(1)} %get-tuple-element.206, f32[16,128,512]{2,1,0:T(8,128)} %fusion.39), kind=kCustom, calls=%fused_computation.4.clone.1 | custom fusion | flops 1048576 | bytes 12582976 | tf_op jit(solution)/shard_map/while/body/eval_jaxpr/scatter-add | solution.py:67
  447.7 9.6 %scatter_fusion.2 = f32[32,128,512]{2,1,0:T(8,128)} fusion(f32[32,128,512]{2,1,0:T(8,128)} %get-tuple-element.240, s32[16]{0:T(128)S(1)} %get-tuple-element.206, f32[16,128,512]{2,1,0:T(8,128)} %fusion.39), kind=kCustom, calls=%fused_computation.4.clone.1 | custom fusion | flops 1048576 | bytes 12582976 | tf_op jit(solution)/shard_map/while/body/eval_jaxpr/scatter-add | solution.py:67
  462.9 9.6 %scatter_fusion.2 = f32[32,128,512]{2,1,0:T(8,128)} fusion(f32[32,128,512]{2,1,0:T(8,128)} %get-tuple-element.240, s32[16]{0:T(128)S(1)} %get-tuple-element.206, f32[16,128,512]{2,1,0:T(8,128)} %fusion.39), kind=kCustom, calls=%fused_computation.4.clone.1 | custom fusion | flops 1048576 | bytes 12582976 | tf_op jit(solution)/shard_map/while/body/eval_jaxpr/scatter-add | solution.py:67
  474.4 138.3 %all-reduce.3.cloned.1.call-done = f32[512,512]{1,0:T(8,128)} async-done(((f32[512,512]{1,0:T(8,128)}), f32[512,512]{1,0:T(8,128)}) %all-reduce.3.cloned.1.call-update) | async-done | bytes 1048592 | tf_op jit(solution)/shard_map/psum | solution.py:54
  615.0 154.3 %reduce-scatter.5.cloned.1.call-done = f32[128,512]{1,0:T(8,128)} async-done(((f32[4096,512]{1,0:T(8,128)}), f32[128,512]{1,0:T(8,128)}) %reduce-scatter.5.cloned.1.call-update) | async-done | bytes 262160 | tf_op jit(solution)/shard_map/reduce_scatter | solution.py:75
  (134 shorter events, 175.8 us)
Async XLA Ops:
  7.2 263.1 %copy-start = (bf16[512,512]{1,0:T(8,128)(2,1)S(1)}, bf16[512,512]{1,0:T(8,128)(2,1)}, u32[]{:S(2)}) copy-start(bf16[512,512]{1,0:T(8,128)(2,1)} %param.12) | copy-start | bytes 1572868
  7.2 92.2 %all-gather.3.cloned.1.call-start = ((), (), s32[]{:S(2)}) async-start(), calls=%async_computation.2 | async-start | bytes 4325376 | tf_op jit(solution)/shard_map/all_gather | solution.py:25
  7.9 294.6 %reduce-scatter.3.cloned.1.call-start = ((), (), s32[]{:S(2)}) async-start(), calls=%async_computation.3 | async-start | bytes 2359296 | tf_op jit(solution)/shard_map/reduce_scatter | solution.py:43
  99.7 151.5 %copy-start.4 = (u32[256]{0:T(256)S(1)}, u32[256]{0:T(256)}, u32[]{:S(2)}) copy-start(u32[256]{0:T(256)} %constant.52) | copy-start | bytes 3076
  99.7 170.6 %copy-start.3 = (bf16[1,1,128,512]{3,2,1,0:T(8,128)(2,1)S(1)}, bf16[1,1,128,512]{3,2,1,0:T(8,128)(2,1)}, u32[]{:S(2)}) copy-start(bf16[1,1,128,512]{3,2,1,0:T(8,128)(2,1)} %param.13) | copy-start | bytes 393220
  249.7 1.4 copy-start.1
  251.1 95.3 %all-gather.5.cloned.1.call-start = ((), (), s32[]{:S(2)}) async-start(), calls=%async_computation.5 | async-start | bytes 1179648 | tf_op jit(solution)/shard_map/all_gather | solution.py:59
  271.3 341.4 %all-reduce.3.cloned.1.call-start = ((), (), s32[]{:S(2)}) async-start(), calls=%async_computation.4 | async-start | bytes 2097152 | tf_op jit(solution)/shard_map/psum | solution.py:54
  304.8 464.5 %reduce-scatter.5.cloned.1.call-start = ((), (), s32[]{:S(2)}) async-start(), calls=%async_computation.6 | async-start | bytes 8650752 | tf_op jit(solution)/shard_map/reduce_scatter | solution.py:75
  472.5 0.9 copy-start.2
Sparse Core Ops, SparseCore 0:
  10.8 88.5 all-gather.2
  251.2 51.2 reduce-scatter.2
  304.9 41.4 all-gather.4
  352.3 260.3 all-reduce.2
  616.9 152.3 reduce-scatter.4
where the time goes:
time: 781 us; the launch traced here: 777 us
  waiting for transfers between devices  443 us (57%)
  other arithmetic  152 us (19%)
  local copies, waits for them, and re-layouts  80.3 us (10%)
  matrix products  68.3 us (9%)
  blocking collectives  17.8 us (2%)
  between operations  15.1 us (2%)
    reduce_scatter x1, waiting for transfers between devices, per_device(): lax.psum_scatter(grad_term, 'row', scatter_dimension=0, tiled=True)  154 us
    psum x1, waiting for transfers between devices, per_device(): weight_grad = lax.psum(weight_term, ('row', 'col')) * nodes ** (-0.5)  138 us
    scatter-add x8, other arithmetic, backward_step(): return (back.at[cid].add(prod), None)  76.7 us
    all_gather x1, waiting for transfers between devices, per_device(): lax.all_gather(features, 'row', axis=1, tiled=True)  76.6 us
    scatter-add x8, other arithmetic, forward_step(): total = total.at[rid].add(prod)  49.2 us
    all_gather x1, waiting for transfers between devices, per_device(): scaled = lax.all_gather(scaled_own, 'col', axis=0, tiled=True)  41.5 us
    dot_general x8, matrix products, forward_step(): jnp.einsum('gij,gjf->gif', block, panel[cid], preferred_element_type=jnp....  34.5 us
    gather x8, local copies, waits for them, and re-layouts, forward_step(): panel[cid]  33.8 us
  transfers between devices with their start and end apart: 5, of which 5 were waited for; matrix products, arithmetic and copies ran while one was open for 19% of the time, Pallas kernels for 0%

commit v1 on v0

v1 whole, which is shorter than its diff:
```python
import jax
import jax.numpy as jnp
from jax import lax
from jax.sharding import PartitionSpec as P


def per_device(features, weight, cotangent, tile_vals, tile_rows, tile_cols, tile_count):
    sub_rows = features.shape[2]
    width = features.shape[3]
    slots = tile_vals.shape[2]
    tile = tile_vals.shape[3]
    rows_axis = lax.axis_size("row")
    cols_axis = lax.axis_size("col")
    tile_rows_blk = sub_rows * cols_axis // tile
    tile_cols_blk = sub_rows * rows_axis // tile
    places = tile_rows_blk * tile_cols_blk

    live = jnp.arange(slots, dtype=jnp.int32) < tile_count[0, 0]
    place = tile_rows[0, 0] * tile_cols_blk + tile_cols[0, 0]
    onehot = (place[:, None] == jnp.arange(places, dtype=jnp.int32)[None, :]) & live[:, None]
    onehot = onehot.astype(jnp.bfloat16).reshape(slots, tile_rows_blk, tile_cols_blk)
    dense = jnp.einsum(
        "kab,kij->aibj", onehot, tile_vals[0, 0], preferred_element_type=jnp.float32
    ).astype(jnp.bfloat16)

    local_deg = jnp.sum(dense.astype(jnp.float32), axis=(2, 3)).reshape(tile_rows_blk * tile)
    deg_own = lax.psum_scatter(local_deg, "col", scatter_dimension=0, tiled=True)
    inv_own = lax.rsqrt(1.0 + deg_own)

    grad_own = cotangent[0, 0]
    projected = lax.dot_general(
        grad_own, weight, (((1,), (1,)), ((), ())), preferred_element_type=jnp.float32
    )
    scaled_own = (inv_own[:, None] * projected).astype(jnp.bfloat16)
    scaled = lax.all_gather(scaled_own, "col", axis=0, tiled=True)
    scaled_tiles = scaled.reshape(tile_rows_blk, tile, width)
    back = jnp.einsum("aibj,aif->bjf", dense, scaled_tiles, preferred_element_type=jnp.float32)
    pieces = back.astype(jnp.bfloat16).reshape(rows_axis, sub_rows, width)
    arrived = lax.all_to_all(pieces, "row", 0, 0)
    ones = jnp.ones((rows_axis,), jnp.bfloat16)
    feature_grad = jnp.einsum(
        "r,rnf->nf", ones, arrived, preferred_element_type=jnp.float32
    ).astype(jnp.bfloat16)

    panel = lax.all_gather(features, "row", axis=1, tiled=True).reshape(tile_cols_blk, tile, width)
    total = jnp.einsum("aibj,bjf->aif", dense, panel, preferred_element_type=jnp.float32)
    partial_agg = total.reshape(tile_rows_blk * tile, width)
    summed = lax.psum_scatter(partial_agg, "col", scatter_dimension=0, tiled=True)
    aggregated = (inv_own[:, None] * summed).astype(jnp.bfloat16)
    layer_out = jnp.dot(aggregated, weight, preferred_element_type=jnp.float32).astype(jnp.bfloat16)
    nodes = sub_rows * rows_axis * cols_axis
    weight_term = lax.dot_general(
        aggregated, grad_own, (((0,), (0,)), ((), ())), preferred_element_type=jnp.float32
    )
    weight_pieces = weight_term.reshape(rows_axis, width // rows_axis, width)
    weight_part = jnp.sum(lax.all_to_all(weight_pieces, "row", 0, 0), axis=0)
    weight_part = lax.psum(weight_part, "col")
    weight_grad = lax.all_gather(weight_part, "row", axis=0, tiled=True) * nodes ** (-0.5)
    return (
        layer_out.reshape(1, 1, sub_rows, width),
        weight_grad,
        feature_grad.reshape(1, 1, sub_rows, width),
    )


def solution(mesh):
    return jax.shard_map(
        per_device,
        mesh=mesh,
        in_specs=(
            P("col", "row", None, None),
            P(),
            P("row", "col", None, None),
            P("row", "col", None, None, None),
            P("row", "col", None),
            P("row", "col", None),
            P("row", "col"),
        ),
        out_specs=(P("row", "col", None, None), P(), P("col", "row", None, None)),
        check_vma=False,
    )
```

time: 781 us -> 367 us (0.47)
  waiting for transfers between devices: 443 us -> 227 us
  other arithmetic: 152 us -> 4.18 us
  local copies, waits for them, and re-layouts: 80.3 us -> 1.4 us
  blocking collectives: 17.8 us -> 54.6 us
  matrix products: 68.3 us -> 44.4 us
  starting transfers between devices: 0.2 us -> 18 us
    reduce_scatter x1 -> x0, waiting for transfers between devices: 154 us -> none  [per_device(): lax.psum_scatter(grad_term, 'row', scatter_dimension=0, tiled=True)]
    psum x1 -> x0, waiting for transfers between devices: 138 us -> none  [per_device(): weight_grad = lax.psum(weight_term, ('row', 'col')) * nodes ** (-0.5)]
    scatter-add x24 -> x0, other arithmetic: 131 us -> none  [the longest x8 76.7 us: backward_step(): return (back.at[cid].add(prod), None)]
    all_to_all x0 -> x2, waiting for transfers between devices: none -> 60.8 us  [the longest x1 60.8 us: per_device(): arrived = lax.all_to_all(pieces, 'row', 0, 0)]
    gather x16 -> x0, local copies, waits for them, and re-layouts: 49.1 us -> none  [the longest x8 33.8 us: forward_step(): panel[cid]]
    psum x0 -> x1, blocking collectives: none -> 36.8 us  [per_device(): weight_part = lax.psum(weight_part, 'col')]
    dot_general x16 -> x4, matrix products: 64.1 us -> 41.2 us  [the longest x1 14.8 us: per_device(): jnp.einsum('kab,kij->aibj', onehot, tile_vals[0, 0], preferred_element_ty...]
    all_gather x0 -> x1, waiting for transfers between devices: none -> 20.3 us  [per_device(): lax.all_gather(weight_part, 'row', axis=0, tiled=True) * nodes ** (-0.5)]
  transfers between devices with their start and end apart: 5 -> 6, of which waited for: 5 -> 5; matrix products, arithmetic and copies ran while one was open for 19% -> 11% of each run, Pallas kernels for 0% -> 0%
where the time goes in v1:
time: 367 us; the launch traced here: 365 us
  waiting for transfers between devices  227 us (62%)
  blocking collectives  54.6 us (15%)
  matrix products  44.4 us (12%)
  starting transfers between devices  18 us (5%)
  between operations  15.1 us (4%)
  other arithmetic  4.18 us (1%)
    all_gather x1, waiting for transfers between devices, per_device(): lax.all_gather(features, 'row', axis=1, tiled=True)  75.3 us
    all_to_all x1, waiting for transfers between devices, per_device(): arrived = lax.all_to_all(pieces, 'row', 0, 0)  60.8 us
    all_gather x1, waiting for transfers between devices, per_device(): scaled = lax.all_gather(scaled_own, 'col', axis=0, tiled=True)  38.6 us
    psum x1, blocking collectives, per_device(): weight_part = lax.psum(weight_part, 'col')  36.8 us
    reduce_scatter x1, waiting for transfers between devices, per_device(): lax.psum_scatter(partial_agg, 'col', scatter_dimension=0, tiled=True)  31.2 us
    all_gather x1, waiting for transfers between devices, per_device(): lax.all_gather(weight_part, 'row', axis=0, tiled=True) * nodes ** (-0.5)  20.3 us
    unnamed x1, blocking collectives  17.9 us
    dot_general x1, matrix products, per_device(): jnp.einsum('kab,kij->aibj', onehot, tile_vals[0, 0], preferred_element_ty...  14.8 us
  transfers between devices with their start and end apart: 6, of which 5 were waited for; matrix products, arithmetic and copies ran while one was open for 11% of the time, Pallas kernels for 0%

profile of v1, /device:TPU:2, one launch (start us, length us, event | category | flops | bytes accessed | tf_op | source)
XLA Modules:
  0.0 364.7 jit_solution(4789647268140108644)
XLA Ops:
  7.2 0.7 all-gather.4.cloned.1.call-update
  8.6 0.7 add_bitcast_fusion
  9.3 14.8 %convert_reduce_fusion = (f32[8,128]{1,0:T(8,128)S(1)}, bf16[8,32,128,128]{3,1,2,0:T(8,128)(2,1)}) fusion(bf16[128,128,128]{2,1,0:T(8,128)(2,1)} %bitcast.63, s32[8,32]{1,0:T(8,128)S(1)} %multiply_add_fusion, s32[128]{0:T(128)S(1)} %add_bitcast_fusion, pred[128]{0:T(512)(128)(4,1)S(1)} %iota_compare_fusion), kind=kOutput, calls=%fused_computation | convolution fusion | flops 1086389248 | bytes 12588672 | tf_op jit(solution)/shard_map/kab,kij->aibj/dot_general | solution.py:22
  24.1 75.3 %all-gather.4.cloned.1.call-done = bf16[1,32,128,512]{3,2,0,1:T(8,128)(2,1)} async-done(((bf16[1,1,128,512]{3,2,0,1:T(8,128)(2,1)}), bf16[1,32,128,512]{3,2,0,1:T(8,128)(2,1)}) %all-gather.4.cloned.1.call-update) | async-done | bytes 4194320 | tf_op jit(solution)/shard_map/all_gather | solution.py:45
  99.4 9.3 %fusion.11 = f32[1024,512]{1,0:T(8,128)} fusion(bf16[1,32,128,512]{3,2,0,1:T(8,128)(2,1)} %all-gather.4.cloned.1.call-done, bf16[1024,32,128]{2,1,0:T(8,128)(2,1)} %bitcast.61), kind=kOutput, calls=%fused_computation.12 | convolution fusion | flops 4294967296 | bytes 14680064 | tf_op jit(solution)/shard_map/aibj,bjf->aif/dot_general | solution.py:46
  108.8 0.6 dynamic-slice
  110.0 17.9 %all-reduce = f32[1024]{0:T(1024)S(1)} all-reduce(f32[1024]{0:T(1024)S(1)} %bitcast.67), channel_id=2, replica_groups=mesh['row'=32,'col'=8] {'col'}, use_global_device_ids=true, to_apply=%region_1.0.clone | all-reduce | flops 1024 | bytes 8192
  127.9 0.1 fusion.28
  128.0 1.0 fusion.16
  129.0 31.2 %reduce-scatter.2.cloned.1.call-done = f32[128,512]{1,0:T(8,128)} async-done(((f32[1024,512]{1,0:T(8,128)}), f32[128,512]{1,0:T(8,128)}) %reduce-scatter.2.cloned.1.call-update) | async-done | bytes 262160 | tf_op jit(solution)/shard_map/reduce_scatter | solution.py:48
  160.2 1.0 fusion.31
  161.2 0.1 copy.19
  161.4 1.3 fusion.19
  162.6 9.1 %all-to-all-start = ((f32[32,16,512]{2,1,0:T(8,128)}), f32[32,16,512]{2,1,0:T(8,128)S(1)}, u32[]{:S(2)}, u32[]{:S(2)}) async-start(f32[32,16,512]{2,1,0:T(8,128)} %fusion.19), calls=%async_computation.1 | async-start | bytes 2097152 | tf_op jit(solution)/shard_map/all_to_all | solution.py:56
  171.7 38.6 %all-gather.8.cloned.1.call-done = bf16[1024,512]{1,0:T(8,128)(2,1)} async-done(((bf16[128,512]{1,0:T(8,128)(2,1)}), bf16[1024,512]{1,0:T(8,128)(2,1)}) %all-gather.8.cloned.1.call-update) | async-done | bytes 1048592 | tf_op jit(solution)/shard_map/all_gather | solution.py:35
  210.3 12.5 %bitcast_convert_fusion = bf16[32,128,512]{2,1,0:T(8,128)(2,1)} fusion(bf16[8,128,512,1]{2,1,0,3:T(8,128)(2,1)} %bitcast.68, bf16[8,128,32,128]{3,2,1,0:T(8,128)(2,1)} %bitcast.62), kind=kOutput, calls=%fused_computation.1 | convolution fusion | flops 4297064448 | bytes 13631488 | tf_op jit(solution)/shard_map/aibj,aif->bjf/dot_general | solution.py:37
  222.8 8.7 %all-to-all-start.1 = ((bf16[32,128,512]{2,1,0:T(8,128)(2,1)}), bf16[32,128,512]{2,1,0:T(8,128)(2,1)}, u32[]{:S(2)}, u32[]{:S(2)}) async-start(bf16[32,128,512]{2,1,0:T(8,128)(2,1)} %bitcast_convert_fusion), calls=%async_computation.2 | async-start | bytes 8388608 | tf_op jit(solution)/shard_map/all_to_all | solution.py:39
  231.7 36.8 %psum.7 = f32[16,512]{1,0:T(8,128)} all-reduce(f32[16,512]{1,0:T(8,128)S(1)} %reduce_sum.19), channel_id=1, replica_groups=mesh['row'=32,'col'=8] {'col'}, use_global_device_ids=true, to_apply=%region_4.0 | all-reduce | flops 8192 | bytes 65536 | tf_op jit(solution)/shard_map/psum | solution.py:57
  268.5 60.8 %all-to-all-done.1 = bf16[32,128,512]{2,1,0:T(8,128)(2,1)} async-done(((bf16[32,128,512]{2,1,0:T(8,128)(2,1)}), bf16[32,128,512]{2,1,0:T(8,128)(2,1)}, u32[]{:S(2)}, u32[]{:S(2)}) %all-to-all-start.1) | async-done | bytes 4194336 | tf_op jit(solution)/shard_map/all_to_all | solution.py:39
  329.3 4.6 %fusion.6 = bf16[1,128,512]{2,0,1:T(2,128)(2,1)S(1)} fusion(bf16[32,128,512]{2,1,0:T(8,128)(2,1)} %all-to-all-done.1), kind=kOutput, calls=%fused_computation.9 | convolution fusion | flops 4194304 | bytes 4325376 | tf_op jit(solution)/shard_map/r,rnf->nf/dot_general | solution.py:41
  333.9 0.7 copy.44
  334.6 0.9 fusion.17
  335.6 20.3 %all-gather.6.cloned.1.call-done = f32[512,512]{1,0:T(8,128)} async-done(((f32[16,512]{1,0:T(8,128)}), f32[512,512]{1,0:T(8,128)}) %all-gather.6.cloned.1.call-update) | async-done | bytes 1048592 | tf_op jit(solution)/shard_map/all_gather | solution.py:58
  355.9 2.3 broadcast_multiply_fusion
  (19 shorter events, 0.3 us)
Async XLA Ops:
  7.2 120.8 %copy-start = (bf16[512,512]{1,0:T(8,128)(2,1)S(1)}, bf16[512,512]{1,0:T(8,128)(2,1)}, u32[]{:S(2)}) copy-start(bf16[512,512]{1,0:T(8,128)(2,1)} %param.8) | copy-start | bytes 1572868
  7.2 92.2 %all-gather.4.cloned.1.call-start = ((), (), s32[]{:S(2)}) async-start(), calls=%async_computation.3 | async-start | bytes 4325376 | tf_op jit(solution)/shard_map/all_gather | solution.py:45
  7.9 152.3 %reduce-scatter.2.cloned.1.call-start = ((), (), s32[]{:S(2)}) async-start(), calls=%async_computation.4 | async-start | bytes 2359296 | tf_op jit(solution)/shard_map/reduce_scatter | solution.py:48
  99.4 9.4 %copy-start.3 = (u32[256]{0:T(256)S(1)}, u32[256]{0:T(256)}, u32[]{:S(2)}) copy-start(u32[256]{0:T(256)} %constant.19) | copy-start | bytes 3076
  99.4 28.6 %copy-start.2 = (bf16[1,1,128,512]{3,2,1,0:T(8,128)(2,1)S(1)}, bf16[1,1,128,512]{3,2,1,0:T(8,128)(2,1)}, u32[]{:S(2)}) copy-start(bf16[1,1,128,512]{3,2,1,0:T(8,128)(2,1)} %param.9) | copy-start | bytes 393220
  108.7 101.6 %all-gather.8.cloned.1.call-start = ((), (), s32[]{:S(2)}) async-start(), calls=%async_computation.6 | async-start | bytes 1179648 | tf_op jit(solution)/shard_map/all_gather | solution.py:35
  162.6 60.2 %all-to-all-start = ((f32[32,16,512]{2,1,0:T(8,128)}), f32[32,16,512]{2,1,0:T(8,128)S(1)}, u32[]{:S(2)}, u32[]{:S(2)}) async-start(f32[32,16,512]{2,1,0:T(8,128)} %fusion.19), calls=%async_computation.1 | async-start | bytes 2097152 | tf_op jit(solution)/shard_map/all_to_all | solution.py:56
  222.8 106.5 %all-to-all-start.1 = ((bf16[32,128,512]{2,1,0:T(8,128)(2,1)}), bf16[32,128,512]{2,1,0:T(8,128)(2,1)}, u32[]{:S(2)}, u32[]{:S(2)}) async-start(bf16[32,128,512]{2,1,0:T(8,128)(2,1)} %bitcast_convert_fusion), calls=%async_computation.2 | async-start | bytes 8388608 | tf_op jit(solution)/shard_map/all_to_all | solution.py:39
  231.6 103.1 %copy-start.1 = (f32[128,512]{1,0:T(8,128)S(1)}, f32[128,512]{1,0:T(8,128)}, u32[]{:S(2)}) copy-start(f32[128,512]{1,0:T(8,128)} %reduce-scatter.2.cloned.1.call-done) | copy-start | bytes 786436
  231.6 124.3 %all-gather.6.cloned.1.call-start = ((), (), s32[]{:S(2)}) async-start(), calls=%async_computation.5 | async-start | bytes 1081344 | tf_op jit(solution)/shard_map/all_gather | solution.py:58
Sparse Core Ops, SparseCore 0:
  10.8 88.5 all-gather.3
  108.8 51.3 reduce-scatter.1
  162.6 47.6 all-gather.7
  268.6 87.2 all-gather.5

commit v2 on v1

--- a/solution.py
+++ b/solution.py
@@ -24,15 +24,17 @@
     ).astype(jnp.bfloat16)
 
     local_deg = jnp.sum(dense.astype(jnp.float32), axis=(2, 3)).reshape(tile_rows_blk * tile)
-    deg_own = lax.psum_scatter(local_deg, "col", scatter_dimension=0, tiled=True)
-    inv_own = lax.rsqrt(1.0 + deg_own)
+    deg_all = lax.psum(local_deg, "col")
+    inv_all = lax.rsqrt(1.0 + deg_all)
+    me_col = lax.axis_index("col")
+    inv_own = lax.dynamic_slice_in_dim(inv_all, me_col * sub_rows, sub_rows)
 
     grad_own = cotangent[0, 0]
+    grad_rows = lax.all_gather(grad_own, "col", axis=0, tiled=True)
     projected = lax.dot_general(
-        grad_own, weight, (((1,), (1,)), ((), ())), preferred_element_type=jnp.float32
+        grad_rows, weight, (((1,), (1,)), ((), ())), preferred_element_type=jnp.float32
     )
-    scaled_own = (inv_own[:, None] * projected).astype(jnp.bfloat16)
-    scaled = lax.all_gather(scaled_own, "col", axis=0, tiled=True)
+    scaled = (inv_all[:, None] * projected).astype(jnp.bfloat16)
     scaled_tiles = scaled.reshape(tile_rows_blk, tile, width)
     back = jnp.einsum("aibj,aif->bjf", dense, scaled_tiles, preferred_element_type=jnp.float32)
     pieces = back.astype(jnp.bfloat16).reshape(rows_axis, sub_rows, width)
@@ -42,7 +44,9 @@
         "r,rnf->nf", ones, arrived, preferred_element_type=jnp.float32
     ).astype(jnp.bfloat16)
 
+    features, _ = lax.optimization_barrier((features, grad_rows))
     panel = lax.all_gather(features, "row", axis=1, tiled=True).reshape(tile_cols_blk, tile, width)
+    panel, _ = lax.optimization_barrier((panel, arrived))
     total = jnp.einsum("aibj,bjf->aif", dense, panel, preferred_element_type=jnp.float32)
     partial_agg = total.reshape(tile_rows_blk * tile, width)
     summed = lax.psum_scatter(partial_agg, "col", scatter_dimension=0, tiled=True)
@@ -54,8 +58,12 @@
     )
     weight_pieces = weight_term.reshape(rows_axis, width // rows_axis, width)
     weight_part = jnp.sum(lax.all_to_all(weight_pieces, "row", 0, 0), axis=0)
-    weight_part = lax.psum(weight_part, "col")
-    weight_grad = lax.all_gather(weight_part, "row", axis=0, tiled=True) * nodes ** (-0.5)
+    weight_pieces = weight_part.reshape(cols_axis, width // rows_axis // cols_axis, width)
+    weight_part = jnp.sum(lax.all_to_all(weight_pieces, "col", 0, 0), axis=0) * nodes ** (-0.5)
+    spread = jnp.broadcast_to(weight_part[None], (cols_axis,) + weight_part.shape)
+    weight_part = lax.all_to_all(spread, "col", 0, 0).reshape(width // rows_axis, width)
+    spread = jnp.broadcast_to(weight_part[None], (rows_axis,) + weight_part.shape)
+    weight_grad = lax.all_to_all(spread, "row", 0, 0).reshape(width, width)
     return (
         layer_out.reshape(1, 1, sub_rows, width),
         weight_grad,

time: 367 us -> 361 us (0.984)
  waiting for transfers between devices: 227 us -> 194 us
  blocking collectives: 54.6 us -> 76.6 us
  matrix products: 44.4 us -> 54.5 us
  starting transfers between devices: 18 us -> 13.4 us
    all_to_all x0 -> x3, blocking collectives: none -> 57.9 us  [the longest x1 39 us: per_device(): weight_part = jnp.sum(lax.all_to_all(weight_pieces, 'row', 0, 0), axis=0)]
    all_gather x2 -> x1, waiting for transfers between devices: 58.9 us -> 10.3 us  [per_device(): grad_rows = lax.all_gather(grad_own, 'col', axis=0, tiled=True)]
    all_to_all x1, waiting for transfers between devices: 60.8 us -> 21.6 us  [per_device(): arrived = lax.all_to_all(pieces, 'row', 0, 0)]
    all_to_all x1, waiting for transfers between devices: 0.01 us -> 23.7 us  [per_device(): weight_grad = lax.all_to_all(spread, 'row', 0, 0).reshape(width, width)]
    reduce_scatter x1, waiting for transfers between devices: 31.2 us -> 51.9 us  [per_device(): lax.psum_scatter(partial_agg, 'col', scatter_dimension=0, tiled=True)]
    psum x1, blocking collectives: 36.8 us -> 18.7 us  [per_device(): deg_all = lax.psum(local_deg, 'col')]
    unnamed x1 -> x0, blocking collectives: 17.9 us -> none
    all_gather x1, waiting for transfers between devices: 75.3 us -> 85.5 us  [per_device(): lax.all_gather(features, 'row', axis=1, tiled=True)]
  transfers between devices with their start and end apart: 6 -> 5, of which waited for: 5 -> 5; matrix products, arithmetic and copies ran while one was open for 11% -> 13% of each run, Pallas kernels for 0% -> 0%
where the time goes in v2:
time: 361 us; the launch traced here: 358 us
  waiting for transfers between devices  194 us (54%)
  blocking collectives  76.6 us (21%)
  matrix products  54.5 us (15%)
  between operations  14.5 us (4%)
  starting transfers between devices  13.4 us (4%)
    all_gather x1, waiting for transfers between devices, per_device(): lax.all_gather(features, 'row', axis=1, tiled=True)  85.5 us
    reduce_scatter x1, waiting for transfers between devices, per_device(): lax.psum_scatter(partial_agg, 'col', scatter_dimension=0, tiled=True)  51.9 us
    all_to_all x1, blocking collectives, per_device(): weight_part = jnp.sum(lax.all_to_all(weight_pieces, 'row', 0, 0), axis=0)  39 us
    all_to_all x1, waiting for transfers between devices, per_device(): weight_grad = lax.all_to_all(spread, 'row', 0, 0).reshape(width, width)  23.7 us
    dot_general x1, matrix products, per_device(): jnp.einsum('aibj,aif->bjf', dense, scaled_tiles, preferred_element_type=j...  22.7 us
    all_to_all x1, waiting for transfers between devices, per_device(): arrived = lax.all_to_all(pieces, 'row', 0, 0)  21.6 us
    psum x1, blocking collectives, per_device(): deg_all = lax.psum(local_deg, 'col')  18.7 us
    dot_general x1, matrix products, per_device(): jnp.einsum('kab,kij->aibj', onehot, tile_vals[0, 0], preferred_element_ty...  14.7 us
  transfers between devices with their start and end apart: 5, of which 5 were waited for; matrix products, arithmetic and copies ran while one was open for 13% of the time, Pallas kernels for 0%

profile of v2, /device:TPU:2, one launch (start us, length us, event | category | flops | bytes accessed | tf_op | source)
XLA Modules:
  0.0 358.2 jit_solution(15065751914351055652)
XLA Ops:
  7.2 0.7 all-gather.6.cloned.1.call-update
  8.0 0.7 all-gather.4.cloned.1.call-update
  9.3 0.7 add_bitcast_fusion
  10.0 14.7 %convert_reduce_fusion = (f32[8,128]{1,0:T(8,128)S(1)}, bf16[8,128,32,128]{3,2,1,0:T(8,128)(2,1)}) fusion(bf16[128,128,128]{2,1,0:T(8,128)(2,1)} %bitcast.62, s32[8,32]{1,0:T(8,128)S(1)} %multiply_add_fusion, s32[128]{0:T(128)S(1)} %add_bitcast_fusion, pred[128]{0:T(512)(128)(4,1)S(1)} %iota_compare_fusion), kind=kOutput, calls=%fused_computation | convolution fusion | flops 1086389248 | bytes 12588672 | tf_op jit(solution)/shard_map/kab,kij->aibj/dot_general | solution.py:22
  24.8 18.7 %psum.7 = f32[1024]{0:T(1024)S(1)} all-reduce(f32[1024]{0:T(1024)S(1)} %bitcast.67), channel_id=1, replica_groups=mesh['row'=32,'col'=8] {'col'}, use_global_device_ids=true, to_apply=%region_1.0 | all-reduce | flops 1024 | bytes 8192 | tf_op jit(solution)/shard_map/psum | solution.py:27
  43.5 10.3 %all-gather.6.cloned.1.call-done = bf16[1,1,1024,512]{3,2,1,0:T(8,128)(2,1)} async-done(((bf16[1,1,128,512]{3,2,1,0:T(8,128)(2,1)}), bf16[1,1,1024,512]{3,2,1,0:T(8,128)(2,1)}) %all-gather.6.cloned.1.call-update) | async-done | bytes 1048592 | tf_op jit(solution)/shard_map/all_gather | solution.py:33
  53.8 2.0 multiply_convert_fusion
  55.8 22.7 %bitcast_convert_fusion = bf16[32,128,512]{2,1,0:T(8,128)(2,1)} fusion(bf16[8,128,512,1]{2,1,0,3:T(8,128)(2,1)S(1)} %bitcast.69, bf16[8,128,32,128]{3,2,1,0:T(8,128)(2,1)} %get-tuple-element.8), kind=kOutput, calls=%fused_computation.1 | convolution fusion | flops 4297064448 | bytes 13631488 | tf_op jit(solution)/shard_map/aibj,aif->bjf/dot_general | solution.py:39
  78.5 9.1 %all-to-all-start = ((bf16[32,128,512]{2,1,0:T(8,128)(2,1)}), bf16[32,128,512]{2,1,0:T(8,128)(2,1)}, u32[]{:S(2)}, u32[]{:S(2)}) async-start(bf16[32,128,512]{2,1,0:T(8,128)(2,1)} %bitcast_convert_fusion), calls=%async_computation | async-start | bytes 8388608 | tf_op jit(solution)/shard_map/all_to_all | solution.py:41
  87.8 85.5 %all-gather.4.cloned.1.call-done = bf16[1,32,128,512]{3,2,0,1:T(8,128)(2,1)} async-done(((bf16[1,1,128,512]{3,2,0,1:T(8,128)(2,1)}), bf16[1,32,128,512]{3,2,0,1:T(8,128)(2,1)}) %all-gather.4.cloned.1.call-update) | async-done | bytes 4194320 | tf_op jit(solution)/shard_map/all_gather | solution.py:48
  173.3 21.6 %all-to-all-done = bf16[32,128,512]{2,1,0:T(8,128)(2,1)} async-done(((bf16[32,128,512]{2,1,0:T(8,128)(2,1)}), bf16[32,128,512]{2,1,0:T(8,128)(2,1)}, u32[]{:S(2)}, u32[]{:S(2)}) %all-to-all-start) | async-done | bytes 4194336 | tf_op jit(solution)/shard_map/all_to_all | solution.py:41
  194.9 9.3 %fusion = f32[8,128,512,1]{2,1,3,0:T(8,128)} fusion(bf16[8,128,32,128]{3,2,1,0:T(8,128)(2,1)} %get-tuple-element.8, bf16[32,128,512]{2,1,0:T(8,128)(2,1)} %bitcast.68), kind=kOutput, calls=%fused_computation.2 | convolution fusion | flops 4294967296 | bytes 14680064 | tf_op jit(solution)/shard_map/aibj,bjf->aif/dot_general | solution.py:50
  204.2 51.9 %reduce-scatter.2.cloned.1.call-done = f32[128,512]{1,0:T(8,128)} async-done(((f32[1024,512]{1,0:T(8,128)}), f32[128,512]{1,0:T(8,128)}) %reduce-scatter.2.cloned.1.call-update) | async-done | bytes 262160 | tf_op jit(solution)/shard_map/reduce_scatter | solution.py:52
  256.2 1.0 fusion.24
  257.6 39.0 %all_to_all.25 = f32[32,16,512]{2,1,0:T(8,128)S(1)} all-to-all(f32[32,16,512]{2,1,0:T(8,128)S(1)} %fusion.13), channel_id=1, replica_groups=mesh['row'=32,'col'=8] {'row'}, dimensions={0} | all-to-all | bytes 2097152 | tf_op jit(solution)/shard_map/all_to_all | solution.py:60
  296.8 10.2 %all_to_all.26 = f32[8,2,512]{2,1,0:T(2,128)S(1)} all-to-all(f32[8,2,512]{2,1,0:T(2,128)S(1)} %reshape.84), channel_id=1, replica_groups=mesh['row'=32,'col'=8] {'col'}, dimensions={0} | all-to-all | bytes 65536 | tf_op jit(solution)/shard_map/all_to_all | solution.py:62
  307.1 8.6 %all_to_all.27 = f32[8,2,512]{2,1,0:T(2,128)S(1)} all-to-all(f32[8,2,512]{2,1,0:T(2,128)S(1)} %broadcast_in_dim.8), channel_id=1, replica_groups=mesh['row'=32,'col'=8] {'col'}, dimensions={0} | all-to-all | bytes 65536 | tf_op jit(solution)/shard_map/all_to_all | solution.py:64
  315.7 1.1 broadcast_in_dim.10
  316.8 3.9 %all-to-all-start.4 = ((f32[32,16,512]{2,1,0:T(8,128)}), f32[32,16,512]{2,1,0:T(8,128)S(1)}, u32[]{:S(2)}, u32[]{:S(2)}) async-start(f32[32,16,512]{2,1,0:T(8,128)} %broadcast_in_dim.10), calls=%async_computation.5 | async-start | bytes 2097152 | tf_op jit(solution)/shard_map/all_to_all | solution.py:66
  320.8 4.6 %fusion.6 = bf16[1,128,512]{2,0,1:T(2,128)(2,1)S(1)} fusion(bf16[32,128,512]{2,1,0:T(8,128)(2,1)} %all-to-all-done), kind=kOutput, calls=%fused_computation.9 | convolution fusion | flops 4194304 | bytes 4325376 | tf_op jit(solution)/shard_map/r,rnf->nf/dot_general | solution.py:43
  325.4 0.7 copy.53
  326.1 0.9 fusion.11
  327.0 23.7 %all-to-all-done.4 = f32[32,16,512]{2,1,0:T(8,128)S(1)} async-done(((f32[32,16,512]{2,1,0:T(8,128)}), f32[32,16,512]{2,1,0:T(8,128)S(1)}, u32[]{:S(2)}, u32[]{:S(2)}) %all-to-all-start.4) | async-done | bytes 1048608 | tf_op jit(solution)/shard_map/all_to_all | solution.py:66
  350.7 1.0 copy.56
  (22 shorter events, 1.0 us)
Async XLA Ops:
  7.2 46.6 %copy-start = (bf16[512,512]{1,0:T(8,128)(2,1)S(1)}, bf16[512,512]{1,0:T(8,128)(2,1)}, u32[]{:S(2)}) copy-start(bf16[512,512]{1,0:T(8,128)(2,1)} %param.8) | copy-start | bytes 1572868
  7.2 46.6 %all-gather.6.cloned.1.call-start = ((), (), s32[]{:S(2)}) async-start(), calls=%async_computation.8 | async-start | bytes 1179648 | tf_op jit(solution)/shard_map/all_gather | solution.py:33
  7.9 165.4 %all-gather.4.cloned.1.call-start = ((), (), s32[]{:S(2)}) async-start(), calls=%async_computation.6 | async-start | bytes 4325376 | tf_op jit(solution)/shard_map/all_gather | solution.py:48
  78.5 116.4 %all-to-all-start = ((bf16[32,128,512]{2,1,0:T(8,128)(2,1)}), bf16[32,128,512]{2,1,0:T(8,128)(2,1)}, u32[]{:S(2)}, u32[]{:S(2)}) async-start(bf16[32,128,512]{2,1,0:T(8,128)(2,1)} %bitcast_convert_fusion), calls=%async_computation | async-start | bytes 8388608 | tf_op jit(solution)/shard_map/all_to_all | solution.py:41
  87.6 168.6 %reduce-scatter.2.cloned.1.call-start = ((), (), s32[]{:S(2)}) async-start(), calls=%async_computation.7 | async-start | bytes 2359296 | tf_op jit(solution)/shard_map/reduce_scatter | solution.py:52
  194.9 62.5 %copy-start.2 = (bf16[1,1,128,512]{3,2,1,0:T(8,128)(2,1)S(1)}, bf16[1,1,128,512]{3,2,1,0:T(8,128)(2,1)}, u32[]{:S(2)}) copy-start(bf16[1,1,128,512]{3,2,1,0:T(8,128)(2,1)} %param.9) | copy-start | bytes 393220
  296.7 29.4 %copy-start.1 = (f32[128,512]{1,0:T(8,128)S(1)}, f32[128,512]{1,0:T(8,128)}, u32[]{:S(2)}) copy-start(f32[128,512]{1,0:T(8,128)} %reduce-scatter.2.cloned.1.call-done) | copy-start | bytes 786436
  316.8 33.9 %all-to-all-start.4 = ((f32[32,16,512]{2,1,0:T(8,128)}), f32[32,16,512]{2,1,0:T(8,128)S(1)}, u32[]{:S(2)}, u32[]{:S(2)}) async-start(f32[32,16,512]{2,1,0:T(8,128)} %broadcast_in_dim.10), calls=%async_computation.5 | async-start | bytes 2097152 | tf_op jit(solution)/shard_map/all_to_all | solution.py:66
Sparse Core Ops, SparseCore 0:
  9.8 43.9 all-gather.5
  56.6 116.6 all-gather.3
  204.3 51.8 reduce-scatter.1

commit v3 on v2

--- a/solution.py
+++ b/solution.py
@@ -23,8 +23,13 @@
         "kab,kij->aibj", onehot, tile_vals[0, 0], preferred_element_type=jnp.float32
     ).astype(jnp.bfloat16)
 
+    dense_t = jnp.einsum(
+        "kab,kij->bjai", onehot, tile_vals[0, 0], preferred_element_type=jnp.float32
+    ).astype(jnp.bfloat16)
+
     local_deg = jnp.sum(dense.astype(jnp.float32), axis=(2, 3)).reshape(tile_rows_blk * tile)
-    deg_all = lax.psum(local_deg, "col")
+    deg_spread = jnp.broadcast_to(local_deg[None], (cols_axis,) + local_deg.shape)
+    deg_all = jnp.sum(lax.all_to_all(deg_spread, "col", 0, 0), axis=0)
     inv_all = lax.rsqrt(1.0 + deg_all)
     me_col = lax.axis_index("col")
     inv_own = lax.dynamic_slice_in_dim(inv_all, me_col * sub_rows, sub_rows)
@@ -36,7 +41,7 @@
     )
     scaled = (inv_all[:, None] * projected).astype(jnp.bfloat16)
     scaled_tiles = scaled.reshape(tile_rows_blk, tile, width)
-    back = jnp.einsum("aibj,aif->bjf", dense, scaled_tiles, preferred_element_type=jnp.float32)
+    back = jnp.einsum("bjai,aif->bjf", dense_t, scaled_tiles, preferred_element_type=jnp.float32)
     pieces = back.astype(jnp.bfloat16).reshape(rows_axis, sub_rows, width)
     arrived = lax.all_to_all(pieces, "row", 0, 0)
     ones = jnp.ones((rows_axis,), jnp.bfloat16)
@@ -49,13 +54,14 @@
     panel, _ = lax.optimization_barrier((panel, arrived))
     total = jnp.einsum("aibj,bjf->aif", dense, panel, preferred_element_type=jnp.float32)
     partial_agg = total.reshape(tile_rows_blk * tile, width)
+    scaled_partial = (inv_all[:, None] * partial_agg).astype(jnp.bfloat16)
+    weight_term = lax.dot_general(
+        scaled_partial, grad_rows, (((0,), (0,)), ((), ())), preferred_element_type=jnp.float32
+    )
     summed = lax.psum_scatter(partial_agg, "col", scatter_dimension=0, tiled=True)
     aggregated = (inv_own[:, None] * summed).astype(jnp.bfloat16)
     layer_out = jnp.dot(aggregated, weight, preferred_element_type=jnp.float32).astype(jnp.bfloat16)
     nodes = sub_rows * rows_axis * cols_axis
-    weight_term = lax.dot_general(
-        aggregated, grad_own, (((0,), (0,)), ((), ())), preferred_element_type=jnp.float32
-    )
     weight_pieces = weight_term.reshape(rows_axis, width // rows_axis, width)
     weight_part = jnp.sum(lax.all_to_all(weight_pieces, "row", 0, 0), axis=0)
     weight_pieces = weight_part.reshape(cols_axis, width // rows_axis // cols_axis, width)

time: 361 us -> 313 us (0.87)
  blocking collectives: 76.6 us -> 19.6 us
  starting transfers between devices: 13.4 us -> 25.6 us
  waiting for transfers between devices: 194 us -> 186 us
    reduce_scatter x1, waiting for transfers between devices: 51.9 us -> 0.01 us  [per_device(): lax.psum_scatter(partial_agg, 'col', scatter_dimension=0, tiled=True)]
    all_to_all x1 -> x0, blocking collectives: 39 us -> none  [per_device(): weight_part = jnp.sum(lax.all_to_all(weight_pieces, 'row', 0, 0), axis=0)]
    all_to_all x0 -> x2, waiting for transfers between devices: none -> 33.4 us  [the longest x1 29.2 us: per_device(): weight_part = jnp.sum(lax.all_to_all(weight_pieces, 'row', 0, 0), axis=0)]
    psum x1 -> x0, blocking collectives: 18.7 us -> none  [per_device(): deg_all = lax.psum(local_deg, 'col')]
    all_to_all x0 -> x2, starting transfers between devices: none -> 12.1 us  [the longest x1 6.22 us: per_device(): weight_part = jnp.sum(lax.all_to_all(weight_pieces, 'row', 0, 0), axis=0)]
    all_gather x1, waiting for transfers between devices: 10.3 us -> 18.4 us  [per_device(): grad_rows = lax.all_gather(grad_own, 'col', axis=0, tiled=True)]
  transfers between devices with their start and end apart: 5 -> 7, of which waited for: 5 -> 6; matrix products, arithmetic and copies ran while one was open for 13% -> 15% of each run, Pallas kernels for 0% -> 0%
where the time goes in v3:
time: 313 us; the launch traced here: 310 us
  waiting for transfers between devices  186 us (59%)
  matrix products  57 us (18%)
  starting transfers between devices  25.6 us (8%)
  blocking collectives  19.6 us (6%)
  between operations  14.5 us (5%)
  local copies, waits for them, and re-layouts  5.79 us (2%)
    all_gather x1, waiting for transfers between devices, per_device(): lax.all_gather(features, 'row', axis=1, tiled=True)  85.4 us
    all_to_all x1, waiting for transfers between devices, per_device(): weight_part = jnp.sum(lax.all_to_all(weight_pieces, 'row', 0, 0), axis=0)  29.2 us
    all_to_all x1, waiting for transfers between devices, per_device(): weight_grad = lax.all_to_all(spread, 'row', 0, 0).reshape(width, width)  24.6 us
    dot_general x1, matrix products, per_device(): jnp.einsum('bjai,aif->bjf', dense_t, scaled_tiles, preferred_element_type...  22.7 us
    all_to_all x1, waiting for transfers between devices, per_device(): arrived = lax.all_to_all(pieces, 'row', 0, 0)  21.9 us
    all_gather x1, waiting for transfers between devices, per_device(): grad_rows = lax.all_gather(grad_own, 'col', axis=0, tiled=True)  18.4 us
    dot_general x1, matrix products, per_device(): jnp.einsum('kab,kij->aibj', onehot, tile_vals[0, 0], preferred_element_ty...  14.8 us
    all_to_all x1, blocking collectives, per_device(): lax.all_to_all(weight_pieces, 'col', 0, 0)  10.6 us
  transfers between devices with their start and end apart: 7, of which 6 were waited for; matrix products, arithmetic and copies ran while one was open for 15% of the time, Pallas kernels for 0%

profile of v3, /device:TPU:2, one launch (start us, length us, event | category | flops | bytes accessed | tf_op | source)
XLA Modules:
  0.0 310.3 jit_solution(860502961405673716)
XLA Ops:
  9.3 14.8 %convert_reduce_fusion = (f32[8,128]{1,0:T(8,128)S(1)}, bf16[8,32,128,128]{3,1,2,0:T(8,128)(2,1)}) fusion(bf16[128,128,128]{2,1,0:T(8,128)(2,1)} %bitcast.66, s32[8,32]{1,0:T(8,128)S(1)} %multiply_add_fusion, s32[128]{0:T(128)S(1)} %add_bitcast_fusion, pred[128]{0:T(512)(128)(4,1)S(1)} %iota_compare_fusion), kind=kOutput, calls=%fused_computation | convolution fusion | flops 1086389248 | bytes 12588672 | tf_op jit(solution)/shard_map/kab,kij->aibj/dot_general | solution.py:22
  24.6 5.9 %all-to-all-start = ((f32[8,1,1024]{2,1,0:T(1,128)}), f32[8,1,1024]{2,1,0:T(1,128)S(1)}, u32[]{:S(2)}, u32[]{:S(2)}) async-start(f32[8,1,1024]{2,1,0:T(1,128)} %broadcast_in_dim.13), calls=%async_computation | async-start | bytes 65536 | tf_op jit(solution)/shard_map/all_to_all | solution.py:32
  30.6 0.7 all-gather.4.cloned.1.call-update
  31.3 4.2 %all-to-all-done = f32[8,1,1024]{2,1,0:T(1,128)S(1)} async-done(((f32[8,1,1024]{2,1,0:T(1,128)}), f32[8,1,1024]{2,1,0:T(1,128)S(1)}, u32[]{:S(2)}, u32[]{:S(2)}) %all-to-all-start) | async-done | bytes 32800 | tf_op jit(solution)/shard_map/all_to_all | solution.py:32
  35.5 18.4 %all-gather.6.cloned.1.call-done = bf16[1,1,1024,512]{3,2,1,0:T(8,128)(2,1)} async-done(((bf16[1,1,128,512]{3,2,1,0:T(8,128)(2,1)}), bf16[1,1,1024,512]{3,2,1,0:T(8,128)(2,1)}) %all-gather.6.cloned.1.call-update) | async-done | bytes 1048592 | tf_op jit(solution)/shard_map/all_gather | solution.py:38
  53.9 2.0 multiply_convert_fusion.1
  55.8 22.7 %bitcast_convert_fusion = bf16[32,128,512]{2,1,0:T(8,128)(2,1)} fusion(bf16[8,128,512,1]{2,1,0,3:T(8,128)(2,1)S(1)} %bitcast.72, bf16[32,128,8,128]{1,0,3,2:T(8,128)(2,1)} %bitcast.62), kind=kOutput, calls=%fused_computation.1 | convolution fusion | flops 4297064448 | bytes 13631488 | tf_op jit(solution)/shard_map/bjai,aif->bjf/dot_general | solution.py:44
  78.5 9.3 %all-to-all-start.1 = ((bf16[32,128,512]{2,1,0:T(8,128)(2,1)}), bf16[32,128,512]{2,1,0:T(8,128)(2,1)}, u32[]{:S(2)}, u32[]{:S(2)}) async-start(bf16[32,128,512]{2,1,0:T(8,128)(2,1)} %bitcast_convert_fusion), calls=%async_computation.1 | async-start | bytes 8388608 | tf_op jit(solution)/shard_map/all_to_all | solution.py:46
  87.9 85.4 %all-gather.4.cloned.1.call-done = bf16[1,32,128,512]{3,2,0,1:T(8,128)(2,1)} async-done(((bf16[1,1,128,512]{3,2,0,1:T(8,128)(2,1)}), bf16[1,32,128,512]{3,2,0,1:T(8,128)(2,1)}) %all-gather.4.cloned.1.call-update) | async-done | bytes 4194320 | tf_op jit(solution)/shard_map/all_gather | solution.py:53
  173.2 21.9 %all-to-all-done.1 = bf16[32,128,512]{2,1,0:T(8,128)(2,1)} async-done(((bf16[32,128,512]{2,1,0:T(8,128)(2,1)}), bf16[32,128,512]{2,1,0:T(8,128)(2,1)}, u32[]{:S(2)}, u32[]{:S(2)}) %all-to-all-start.1) | async-done | bytes 4194336 | tf_op jit(solution)/shard_map/all_to_all | solution.py:46
  195.1 7.8 %fusion = f32[8,128,512,1]{2,1,3,0:T(8,128)S(1)} fusion(bf16[8,128,32,128]{3,2,1,0:T(8,128)(2,1)} %bitcast.63, bf16[32,128,512]{2,1,0:T(8,128)(2,1)} %bitcast.71), kind=kOutput, calls=%fused_computation.2 | convolution fusion | flops 4294967296 | bytes 14680064 | tf_op jit(solution)/shard_map/aibj,bjf->aif/dot_general | solution.py:55
  203.0 1.3 fusion.12
  204.3 2.3 copy.39
  206.6 3.2 %fusion.13 = f32[32,16,512]{2,1,0:T(8,128)} fusion(bf16[32,16,1024]{2,1,0:T(8,128)(2,1)} %bitcast.67, bf16[1,1,1024,512]{3,2,1,0:T(8,128)(2,1)} %all-gather.6.cloned.1.call-done), kind=kOutput, calls=%fused_computation.17 | convolution fusion | flops 536870912 | bytes 3145728 | tf_op jit(solution)/shard_map/dot_general | solution.py:58
  209.8 6.2 %all-to-all-start.2 = ((f32[32,16,512]{2,1,0:T(8,128)}), f32[32,16,512]{2,1,0:T(8,128)S(1)}, u32[]{:S(2)}, u32[]{:S(2)}) async-start(f32[32,16,512]{2,1,0:T(8,128)} %fusion.13), calls=%async_computation.3 | async-start | bytes 2097152 | tf_op jit(solution)/shard_map/all_to_all | solution.py:66
  216.8 29.2 %all-to-all-done.2 = f32[32,16,512]{2,1,0:T(8,128)S(1)} async-done(((f32[32,16,512]{2,1,0:T(8,128)}), f32[32,16,512]{2,1,0:T(8,128)S(1)}, u32[]{:S(2)}, u32[]{:S(2)}) %all-to-all-start.2) | async-done | bytes 1048608 | tf_op jit(solution)/shard_map/all_to_all | solution.py:66
  246.1 10.6 %all_to_all.31 = f32[8,2,512]{2,1,0:T(2,128)S(1)} all-to-all(f32[8,2,512]{2,1,0:T(2,128)S(1)} %reshape.91), channel_id=1, replica_groups=mesh['row'=32,'col'=8] {'col'}, dimensions={0} | all-to-all | bytes 65536 | tf_op jit(solution)/shard_map/all_to_all | solution.py:68
  256.8 9.0 %all_to_all.32 = f32[8,2,512]{2,1,0:T(2,128)S(1)} all-to-all(f32[8,2,512]{2,1,0:T(2,128)S(1)} %broadcast_in_dim.14), channel_id=1, replica_groups=mesh['row'=32,'col'=8] {'col'}, dimensions={0} | all-to-all | bytes 65536 | tf_op jit(solution)/shard_map/all_to_all | solution.py:70
  265.8 1.1 broadcast_in_dim.16
  266.9 4.0 %all-to-all-start.5 = ((f32[32,16,512]{2,1,0:T(8,128)}), f32[32,16,512]{2,1,0:T(8,128)S(1)}, u32[]{:S(2)}, u32[]{:S(2)}) async-start(f32[32,16,512]{2,1,0:T(8,128)} %broadcast_in_dim.16), calls=%async_computation.6 | async-start | bytes 2097152 | tf_op jit(solution)/shard_map/all_to_all | solution.py:72
  271.0 4.7 %fusion.6 = bf16[1,128,512]{2,0,1:T(2,128)(2,1)S(1)} fusion(bf16[32,128,512]{2,1,0:T(8,128)(2,1)} %all-to-all-done.1), kind=kOutput, calls=%fused_computation.9 | convolution fusion | flops 4194304 | bytes 4325376 | tf_op jit(solution)/shard_map/r,rnf->nf/dot_general | solution.py:48
  276.3 24.6 %all-to-all-done.5 = f32[32,16,512]{2,1,0:T(8,128)S(1)} async-done(((f32[32,16,512]{2,1,0:T(8,128)}), f32[32,16,512]{2,1,0:T(8,128)S(1)}, u32[]{:S(2)}, u32[]{:S(2)}) %all-to-all-start.5) | async-done | bytes 1048608 | tf_op jit(solution)/shard_map/all_to_all | solution.py:72
  300.9 1.9 fusion.11
  302.8 1.0 copy.68
  (24 shorter events, 3.7 us)
Async XLA Ops:
  7.2 46.7 %copy-start = (bf16[512,512]{1,0:T(8,128)(2,1)S(1)}, bf16[512,512]{1,0:T(8,128)(2,1)}, u32[]{:S(2)}) copy-start(bf16[512,512]{1,0:T(8,128)(2,1)} %param.8) | copy-start | bytes 1572868
  7.2 46.7 %all-gather.6.cloned.1.call-start = ((), (), s32[]{:S(2)}) async-start(), calls=%async_computation.9 | async-start | bytes 1179648 | tf_op jit(solution)/shard_map/all_gather | solution.py:38
  24.6 10.8 %all-to-all-start = ((f32[8,1,1024]{2,1,0:T(1,128)}), f32[8,1,1024]{2,1,0:T(1,128)S(1)}, u32[]{:S(2)}, u32[]{:S(2)}) async-start(f32[8,1,1024]{2,1,0:T(1,128)} %broadcast_in_dim.13), calls=%async_computation | async-start | bytes 65536 | tf_op jit(solution)/shard_map/all_to_all | solution.py:32
  30.6 142.6 %all-gather.4.cloned.1.call-start = ((), (), s32[]{:S(2)}) async-start(), calls=%async_computation.7 | async-start | bytes 4325376 | tf_op jit(solution)/shard_map/all_gather | solution.py:53
  78.5 116.6 %all-to-all-start.1 = ((bf16[32,128,512]{2,1,0:T(8,128)(2,1)}), bf16[32,128,512]{2,1,0:T(8,128)(2,1)}, u32[]{:S(2)}, u32[]{:S(2)}) async-start(bf16[32,128,512]{2,1,0:T(8,128)(2,1)} %bitcast_convert_fusion), calls=%async_computation.1 | async-start | bytes 8388608 | tf_op jit(solution)/shard_map/all_to_all | solution.py:46
  203.0 6.8 %copy-start.1 = (f32[8,128,512,1]{2,1,3,0:T(8,128)}, f32[8,128,512,1]{2,1,3,0:T(8,128)S(1)}, u32[]{:S(2)}) copy-start(f32[8,128,512,1]{2,1,3,0:T(8,128)S(1)} %fusion) | copy-start | bytes 6291460
  209.8 36.2 %all-to-all-start.2 = ((f32[32,16,512]{2,1,0:T(8,128)}), f32[32,16,512]{2,1,0:T(8,128)S(1)}, u32[]{:S(2)}, u32[]{:S(2)}) async-start(f32[32,16,512]{2,1,0:T(8,128)} %fusion.13), calls=%async_computation.3 | async-start | bytes 2097152 | tf_op jit(solution)/shard_map/all_to_all | solution.py:66
  216.0 84.9 %reduce-scatter.2.cloned.1.call-start = ((), (), s32[]{:S(2)}) async-start(), calls=%async_computation.8 | async-start | bytes 2359296 | tf_op jit(solution)/shard_map/reduce_scatter | solution.py:61
  266.9 34.0 %all-to-all-start.5 = ((f32[32,16,512]{2,1,0:T(8,128)}), f32[32,16,512]{2,1,0:T(8,128)S(1)}, u32[]{:S(2)}, u32[]{:S(2)}) async-start(f32[32,16,512]{2,1,0:T(8,128)} %broadcast_in_dim.16), calls=%async_computation.6 | async-start | bytes 2097152 | tf_op jit(solution)/shard_map/all_to_all | solution.py:72
Sparse Core Ops, SparseCore 0:
  9.8 44.0 all-gather.5
  56.6 116.5 all-gather.3
  219.4 64.5 reduce-scatter.1

commit v4 on v3

--- a/solution.py
+++ b/solution.py
@@ -23,10 +23,6 @@
         "kab,kij->aibj", onehot, tile_vals[0, 0], preferred_element_type=jnp.float32
     ).astype(jnp.bfloat16)
 
-    dense_t = jnp.einsum(
-        "kab,kij->bjai", onehot, tile_vals[0, 0], preferred_element_type=jnp.float32
-    ).astype(jnp.bfloat16)
-
     local_deg = jnp.sum(dense.astype(jnp.float32), axis=(2, 3)).reshape(tile_rows_blk * tile)
     deg_spread = jnp.broadcast_to(local_deg[None], (cols_axis,) + local_deg.shape)
     deg_all = jnp.sum(lax.all_to_all(deg_spread, "col", 0, 0), axis=0)
@@ -40,9 +36,11 @@
         grad_rows, weight, (((1,), (1,)), ((), ())), preferred_element_type=jnp.float32
     )
     scaled = (inv_all[:, None] * projected).astype(jnp.bfloat16)
-    scaled_tiles = scaled.reshape(tile_rows_blk, tile, width)
-    back = jnp.einsum("bjai,aif->bjf", dense_t, scaled_tiles, preferred_element_type=jnp.float32)
-    pieces = back.astype(jnp.bfloat16).reshape(rows_axis, sub_rows, width)
+    dense_flat = dense.reshape(tile_rows_blk * tile, tile_cols_blk * tile)
+    back_t = lax.dot_general(
+        scaled, dense_flat, (((0,), (0,)), ((), ())), preferred_element_type=jnp.float32
+    )
+    pieces = back_t.astype(jnp.bfloat16).T.reshape(rows_axis, sub_rows, width)
     arrived = lax.all_to_all(pieces, "row", 0, 0)
     ones = jnp.ones((rows_axis,), jnp.bfloat16)
     feature_grad = jnp.einsum(
@@ -62,14 +60,14 @@
     aggregated = (inv_own[:, None] * summed).astype(jnp.bfloat16)
     layer_out = jnp.dot(aggregated, weight, preferred_element_type=jnp.float32).astype(jnp.bfloat16)
     nodes = sub_rows * rows_axis * cols_axis
-    weight_pieces = weight_term.reshape(rows_axis, width // rows_axis, width)
-    weight_part = jnp.sum(lax.all_to_all(weight_pieces, "row", 0, 0), axis=0)
-    weight_pieces = weight_part.reshape(cols_axis, width // rows_axis // cols_axis, width)
-    weight_part = jnp.sum(lax.all_to_all(weight_pieces, "col", 0, 0), axis=0) * nodes ** (-0.5)
+    weight_pieces = weight_term.reshape(cols_axis, width // cols_axis, width)
+    weight_part = jnp.sum(lax.all_to_all(weight_pieces, "col", 0, 0), axis=0)
+    weight_pieces = weight_part.reshape(rows_axis, width // cols_axis // rows_axis, width)
+    weight_part = jnp.sum(lax.all_to_all(weight_pieces, "row", 0, 0), axis=0) * nodes ** (-0.5)
+    spread = jnp.broadcast_to(weight_part[None], (rows_axis,) + weight_part.shape)
+    weight_part = lax.all_to_all(spread, "row", 0, 0).reshape(width // cols_axis, width)
     spread = jnp.broadcast_to(weight_part[None], (cols_axis,) + weight_part.shape)
-    weight_part = lax.all_to_all(spread, "col", 0, 0).reshape(width // rows_axis, width)
-    spread = jnp.broadcast_to(weight_part[None], (rows_axis,) + weight_part.shape)
-    weight_grad = lax.all_to_all(spread, "row", 0, 0).reshape(width, width)
+    weight_grad = lax.all_to_all(spread, "col", 0, 0).reshape(width, width)
     return (
         layer_out.reshape(1, 1, sub_rows, width),
         weight_grad,

time: 313 us -> 291 us (0.930)
  waiting for transfers between devices: 186 us -> 143 us
  blocking collectives: 19.6 us -> 62.5 us
  matrix products: 57 us -> 43.1 us
  starting transfers between devices: 25.6 us -> 21 us
    all_to_all x2 -> x1, waiting for transfers between devices: 53.8 us -> 8.46 us  [per_device(): weight_grad = lax.all_to_all(spread, 'col', 0, 0).reshape(width, width)]
    all_to_all x2 -> x3, blocking collectives: 19.6 us -> 62.5 us  [the longest x1 31 us: per_device(): weight_part = jnp.sum(lax.all_to_all(weight_pieces, 'col', 0, 0), axis=0)]
    all_gather x1, waiting for transfers between devices: 85.4 us -> 106 us  [per_device(): lax.all_gather(features, 'row', axis=1, tiled=True)]
    all_to_all x1, waiting for transfers between devices: 21.9 us -> 4.23 us  [per_device(): arrived = lax.all_to_all(pieces, 'row', 0, 0)]
    dot_general x2 -> x1, matrix products: 24.6 us -> 10.7 us  [per_device(): lax.dot_general(scaled, dense_flat, (((0,), (0,)), ((), ())), preferred_e...]
    all_to_all x2 -> x1, starting transfers between devices: 10.3 us -> 5.68 us  [per_device(): weight_grad = lax.all_to_all(spread, 'col', 0, 0).reshape(width, width)]
  transfers between devices with their start and end apart: 7 -> 6, of which waited for: 6 -> 5; matrix products, arithmetic and copies ran while one was open for 15% -> 13% of each run, Pallas kernels for 0% -> 0%
where the time goes in v4:
time: 291 us
  waiting for transfers between devices  143 us (49%)
  blocking collectives  62.5 us (21%)
  matrix products  43.1 us (15%)
  starting transfers between devices  21 us (7%)
  between operations  14.5 us (5%)
  local copies, waits for them, and re-layouts  4.19 us (1%)
    all_gather x1, waiting for transfers between devices, per_device(): lax.all_gather(features, 'row', axis=1, tiled=True)  106 us
    all_to_all x1, blocking collectives, per_device(): weight_part = jnp.sum(lax.all_to_all(weight_pieces, 'col', 0, 0), axis=0)  31 us
    all_gather x1, waiting for transfers between devices, per_device(): grad_rows = lax.all_gather(grad_own, 'col', axis=0, tiled=True)  18.4 us
    all_to_all x1, blocking collectives, per_device(): lax.all_to_all(weight_pieces, 'row', 0, 0)  16.6 us
    all_to_all x1, blocking collectives, per_device(): lax.all_to_all(spread, 'row', 0, 0).reshape(width // cols_axis, width)  14.9 us
    dot_general x1, matrix products, per_device(): jnp.einsum('kab,kij->aibj', onehot, tile_vals[0, 0], preferred_element_ty...  14.7 us
    dot_general x1, matrix products, per_device(): lax.dot_general(scaled, dense_flat, (((0,), (0,)), ((), ())), preferred_e...  10.7 us
    dot_general x1, matrix products, per_device(): jnp.einsum('aibj,bjf->aif', dense, panel, preferred_element_type=jnp.floa...  9.25 us
  transfers between devices with their start and end apart: 6, of which 5 were waited for; matrix products, arithmetic and copies ran while one was open for 13% of the time, Pallas kernels for 0%

profile of v4, /device:TPU:2, one launch (start us, length us, event | category | flops | bytes accessed | tf_op | source)
XLA Modules:
  0.0 290.5 jit_solution(3232014950087334249)
XLA Ops:
  7.2 0.7 all-gather.6.cloned.1.call-update
  8.6 0.7 add_bitcast_fusion
  9.3 14.7 %convert_reduce_fusion = (f32[8,128]{1,0:T(8,128)S(1)}, bf16[8,32,128,128]{3,1,2,0:T(8,128)(2,1)}) fusion(bf16[128,128,128]{2,1,0:T(8,128)(2,1)} %bitcast.68, s32[8,32]{1,0:T(8,128)S(1)} %multiply_add_fusion, s32[128]{0:T(128)S(1)} %add_bitcast_fusion, pred[128]{0:T(512)(128)(4,1)S(1)} %iota_compare_fusion), kind=kOutput, calls=%fused_computation | convolution fusion | flops 1086389248 | bytes 12588672 | tf_op jit(solution)/shard_map/kab,kij->aibj/dot_general | solution.py:22
  24.6 5.9 %all-to-all-start = ((f32[8,1,1024]{2,1,0:T(1,128)}), f32[8,1,1024]{2,1,0:T(1,128)S(1)}, u32[]{:S(2)}, u32[]{:S(2)}) async-start(f32[8,1,1024]{2,1,0:T(1,128)} %broadcast_in_dim.13), calls=%async_computation | async-start | bytes 65536 | tf_op jit(solution)/shard_map/all_to_all | solution.py:28
  30.6 0.7 all-gather.4.cloned.1.call-update
  31.3 4.2 %all-to-all-done = f32[8,1,1024]{2,1,0:T(1,128)S(1)} async-done(((f32[8,1,1024]{2,1,0:T(1,128)}), f32[8,1,1024]{2,1,0:T(1,128)S(1)}, u32[]{:S(2)}, u32[]{:S(2)}) %all-to-all-start) | async-done | bytes 32800 | tf_op jit(solution)/shard_map/all_to_all | solution.py:28
  35.5 18.4 %all-gather.6.cloned.1.call-done = bf16[1,1,1024,512]{3,2,1,0:T(8,128)(2,1)} async-done(((bf16[1,1,128,512]{3,2,1,0:T(8,128)(2,1)}), bf16[1,1,1024,512]{3,2,1,0:T(8,128)(2,1)}) %all-gather.6.cloned.1.call-update) | async-done | bytes 1048592 | tf_op jit(solution)/shard_map/all_gather | solution.py:34
  53.9 10.7 %fusion.5 = bf16[4096,512]{1,0:T(8,128)(2,1)} fusion(bf16[128,8,32,128]{3,2,1,0:T(8,128)(2,1)} %bitcast.63, bf16[512,512]{1,0:T(8,128)(2,1)S(1)} %copy-done, f32[1024]{0:T(1024)S(1)} %add_rsqrt_fusion, bf16[1,1,1024,512]{3,2,1,0:T(8,128)(2,1)} %all-gather.6.cloned.1.call-done), kind=kOutput, calls=%fused_computation.7 | convolution fusion | flops 4834983936 | bytes 14159872 | tf_op jit(solution)/shard_map/dot_general | solution.py:40
  64.5 9.1 %all-to-all-start.1 = ((bf16[32,128,512]{2,1,0:T(8,128)(2,1)}), bf16[32,128,512]{2,1,0:T(8,128)(2,1)}, u32[]{:S(2)}, u32[]{:S(2)}) async-start(bf16[32,128,512]{2,1,0:T(8,128)(2,1)} %bitcast.66), calls=%async_computation.1 | async-start | bytes 8388608 | tf_op jit(solution)/shard_map/all_to_all | solution.py:44
  73.9 106.0 %all-gather.4.cloned.1.call-done = bf16[1,32,128,512]{3,2,0,1:T(8,128)(2,1)} async-done(((bf16[1,1,128,512]{3,2,0,1:T(8,128)(2,1)}), bf16[1,32,128,512]{3,2,0,1:T(8,128)(2,1)}) %all-gather.4.cloned.1.call-update) | async-done | bytes 4194320 | tf_op jit(solution)/shard_map/all_gather | solution.py:51
  179.9 4.2 %all-to-all-done.1 = bf16[32,128,512]{2,1,0:T(8,128)(2,1)} async-done(((bf16[32,128,512]{2,1,0:T(8,128)(2,1)}), bf16[32,128,512]{2,1,0:T(8,128)(2,1)}, u32[]{:S(2)}, u32[]{:S(2)}) %all-to-all-start.1) | async-done | bytes 4194336 | tf_op jit(solution)/shard_map/all_to_all | solution.py:44
  184.1 9.2 %fusion.3 = f32[8,128,512,1]{2,1,3,0:T(8,128)} fusion(bf16[8,128,32,128]{3,2,1,0:T(8,128)(2,1)} %bitcast.64, bf16[32,128,512]{2,1,0:T(8,128)(2,1)} %bitcast.73), kind=kOutput, calls=%fused_computation.4 | convolution fusion | flops 4294967296 | bytes 14680064 | tf_op jit(solution)/shard_map/aibj,bjf->aif/dot_general | solution.py:53
  193.4 1.8 fusion.14
  195.8 1.9 fusion.15
  197.7 31.0 %all_to_all.31 = f32[8,64,512]{2,1,0:T(8,128)S(1)} all-to-all(f32[8,64,512]{2,1,0:T(8,128)S(1)} %fusion.15), channel_id=1, replica_groups=mesh['row'=32,'col'=8] {'col'}, dimensions={0} | all-to-all | bytes 2097152 | tf_op jit(solution)/shard_map/all_to_all | solution.py:64
  228.8 16.6 %all_to_all.32 = f32[32,2,512]{2,1,0:T(2,128)S(1)} all-to-all(f32[32,2,512]{2,1,0:T(2,128)S(1)} %reshape.95), channel_id=1, replica_groups=mesh['row'=32,'col'=8] {'row'}, dimensions={0} | all-to-all | bytes 262144 | tf_op jit(solution)/shard_map/all_to_all | solution.py:66
  245.5 14.9 %all_to_all.33 = f32[32,2,512]{2,1,0:T(2,128)S(1)} all-to-all(f32[32,2,512]{2,1,0:T(2,128)S(1)} %broadcast_in_dim.14), channel_id=1, replica_groups=mesh['row'=32,'col'=8] {'row'}, dimensions={0} | all-to-all | bytes 262144 | tf_op jit(solution)/shard_map/all_to_all | solution.py:68
  260.5 1.1 broadcast_in_dim.16
  261.6 5.7 %all-to-all-start.5 = ((f32[8,64,512]{2,1,0:T(8,128)}), f32[8,64,512]{2,1,0:T(8,128)S(1)}, u32[]{:S(2)}, u32[]{:S(2)}) async-start(f32[8,64,512]{2,1,0:T(8,128)} %broadcast_in_dim.16), calls=%async_computation.6 | async-start | bytes 2097152 | tf_op jit(solution)/shard_map/all_to_all | solution.py:70
  267.4 4.6 %fusion.10 = bf16[1,128,512]{2,0,1:T(2,128)(2,1)S(1)} fusion(bf16[32,128,512]{2,1,0:T(8,128)(2,1)} %all-to-all-done.1), kind=kOutput, calls=%fused_computation.10 | convolution fusion | flops 4194304 | bytes 4325376 | tf_op jit(solution)/shard_map/r,rnf->nf/dot_general | solution.py:46
  272.0 0.7 copy.58
  272.7 8.5 %all-to-all-done.5 = f32[8,64,512]{2,1,0:T(8,128)S(1)} async-done(((f32[8,64,512]{2,1,0:T(8,128)}), f32[8,64,512]{2,1,0:T(8,128)S(1)}, u32[]{:S(2)}, u32[]{:S(2)}) %all-to-all-start.5) | async-done | bytes 1048608 | tf_op jit(solution)/shard_map/all_to_all | solution.py:70
  281.1 1.9 fusion.13
  283.0 1.0 copy.61
  (20 shorter events, 1.9 us)
Async XLA Ops:
  7.2 46.7 %copy-start = (bf16[512,512]{1,0:T(8,128)(2,1)S(1)}, bf16[512,512]{1,0:T(8,128)(2,1)}, u32[]{:S(2)}) copy-start(bf16[512,512]{1,0:T(8,128)(2,1)} %param.8) | copy-start | bytes 1572868
  7.2 46.7 %all-gather.6.cloned.1.call-start = ((), (), s32[]{:S(2)}) async-start(), calls=%async_computation.9 | async-start | bytes 1179648 | tf_op jit(solution)/shard_map/all_gather | solution.py:34
  24.6 10.8 %all-to-all-start = ((f32[8,1,1024]{2,1,0:T(1,128)}), f32[8,1,1024]{2,1,0:T(1,128)S(1)}, u32[]{:S(2)}, u32[]{:S(2)}) async-start(f32[8,1,1024]{2,1,0:T(1,128)} %broadcast_in_dim.13), calls=%async_computation | async-start | bytes 65536 | tf_op jit(solution)/shard_map/all_to_all | solution.py:28
  30.6 149.3 %all-gather.4.cloned.1.call-start = ((), (), s32[]{:S(2)}) async-start(), calls=%async_computation.7 | async-start | bytes 4325376 | tf_op jit(solution)/shard_map/all_gather | solution.py:51
  64.5 119.6 %all-to-all-start.1 = ((bf16[32,128,512]{2,1,0:T(8,128)(2,1)}), bf16[32,128,512]{2,1,0:T(8,128)(2,1)}, u32[]{:S(2)}, u32[]{:S(2)}) async-start(bf16[32,128,512]{2,1,0:T(8,128)(2,1)} %bitcast.66), calls=%async_computation.1 | async-start | bytes 8388608 | tf_op jit(solution)/shard_map/all_to_all | solution.py:44
  73.7 207.5 %reduce-scatter.2.cloned.1.call-start = ((), (), s32[]{:S(2)}) async-start(), calls=%async_computation.8 | async-start | bytes 2359296 | tf_op jit(solution)/shard_map/reduce_scatter | solution.py:59
  261.6 19.5 %all-to-all-start.5 = ((f32[8,64,512]{2,1,0:T(8,128)}), f32[8,64,512]{2,1,0:T(8,128)S(1)}, u32[]{:S(2)}, u32[]{:S(2)}) async-start(f32[8,64,512]{2,1,0:T(8,128)} %broadcast_in_dim.16), calls=%async_computation.6 | async-start | bytes 2097152 | tf_op jit(solution)/shard_map/all_to_all | solution.py:70
Sparse Core Ops, SparseCore 0:
  9.8 44.0 all-gather.5
  56.6 123.2 all-gather.3
  193.5 64.3 reduce-scatter.1

commit v5 on v4

--- a/solution.py
+++ b/solution.py
@@ -31,7 +31,8 @@
     inv_own = lax.dynamic_slice_in_dim(inv_all, me_col * sub_rows, sub_rows)
 
     grad_own = cotangent[0, 0]
-    grad_rows = lax.all_gather(grad_own, "col", axis=0, tiled=True)
+    grad_spread = jnp.broadcast_to(grad_own[None], (cols_axis,) + grad_own.shape)
+    grad_rows = lax.all_to_all(grad_spread, "col", 0, 0).reshape(cols_axis * sub_rows, width)
     projected = lax.dot_general(
         grad_rows, weight, (((1,), (1,)), ((), ())), preferred_element_type=jnp.float32
     )
@@ -47,15 +48,15 @@
         "r,rnf->nf", ones, arrived, preferred_element_type=jnp.float32
     ).astype(jnp.bfloat16)
 
-    features, _ = lax.optimization_barrier((features, grad_rows))
     panel = lax.all_gather(features, "row", axis=1, tiled=True).reshape(tile_cols_blk, tile, width)
-    panel, _ = lax.optimization_barrier((panel, arrived))
+    panel, _ = lax.optimization_barrier((panel, pieces))
     total = jnp.einsum("aibj,bjf->aif", dense, panel, preferred_element_type=jnp.float32)
     partial_agg = total.reshape(tile_rows_blk * tile, width)
     scaled_partial = (inv_all[:, None] * partial_agg).astype(jnp.bfloat16)
     weight_term = lax.dot_general(
         scaled_partial, grad_rows, (((0,), (0,)), ((), ())), preferred_element_type=jnp.float32
     )
+    weight_term, _ = lax.optimization_barrier((weight_term, arrived))
     summed = lax.psum_scatter(partial_agg, "col", scatter_dimension=0, tiled=True)
     aggregated = (inv_own[:, None] * summed).astype(jnp.bfloat16)
     layer_out = jnp.dot(aggregated, weight, preferred_element_type=jnp.float32).astype(jnp.bfloat16)

time: 291 us -> 272 us (0.935)
  waiting for transfers between devices: 143 us -> 114 us
  blocking collectives: 62.5 us -> 72.5 us
    all_gather x1, waiting for transfers between devices: 106 us -> 44.4 us  [per_device(): lax.all_gather(features, 'row', axis=1, tiled=True)]
    all_to_all x1, waiting for transfers between devices: 4.23 us -> 47.4 us  [per_device(): arrived = lax.all_to_all(pieces, 'row', 0, 0)]
    all_gather x1 -> x0, waiting for transfers between devices: 18.4 us -> none  [per_device(): grad_rows = lax.all_gather(grad_own, 'col', axis=0, tiled=True)]
    all_to_all x0 -> x1, blocking collectives: none -> 10.6 us  [per_device(): deg_all = jnp.sum(lax.all_to_all(deg_spread, 'col', 0, 0), axis=0)]
    all_to_all x1, waiting for transfers between devices: 4.15 us -> 13.4 us  [per_device(): lax.all_to_all(grad_spread, 'col', 0, 0)]
  transfers between devices with their start and end apart: 6 -> 5, of which waited for: 5 -> 4; matrix products, arithmetic and copies ran while one was open for 13% -> 17% of each run, Pallas kernels for 0% -> 0%
where the time goes in v5:
time: 272 us
  waiting for transfers between devices  114 us (42%)
  blocking collectives  72.5 us (27%)
  matrix products  43.4 us (16%)
  starting transfers between devices  21.9 us (8%)
  between operations  14.8 us (5%)
  local copies, waits for them, and re-layouts  4.11 us (2%)
    all_to_all x1, waiting for transfers between devices, per_device(): arrived = lax.all_to_all(pieces, 'row', 0, 0)  47.4 us
    all_gather x1, waiting for transfers between devices, per_device(): lax.all_gather(features, 'row', axis=1, tiled=True)  44.4 us
    all_to_all x1, blocking collectives, per_device(): weight_part = jnp.sum(lax.all_to_all(weight_pieces, 'col', 0, 0), axis=0)  29.8 us
    all_to_all x1, blocking collectives, per_device(): lax.all_to_all(weight_pieces, 'row', 0, 0)  17.2 us
    all_to_all x1, blocking collectives, per_device(): lax.all_to_all(spread, 'row', 0, 0).reshape(width // cols_axis, width)  14.9 us
    dot_general x1, matrix products, per_device(): jnp.einsum('kab,kij->aibj', onehot, tile_vals[0, 0], preferred_element_ty...  14.8 us
    all_to_all x1, waiting for transfers between devices, per_device(): lax.all_to_all(grad_spread, 'col', 0, 0)  13.4 us
    all_to_all x1, blocking collectives, per_device(): deg_all = jnp.sum(lax.all_to_all(deg_spread, 'col', 0, 0), axis=0)  10.6 us
  transfers between devices with their start and end apart: 5, of which 4 were waited for; matrix products, arithmetic and copies ran while one was open for 17% of the time, Pallas kernels for 0%

profile of v5, /device:TPU:2, one launch (start us, length us, event | category | flops | bytes accessed | tf_op | source)
XLA Modules:
  0.0 271.8 jit_solution(18072402627793912526)
XLA Ops:
  7.2 0.7 all-gather.2.cloned.1.call-update
  8.6 0.7 add_bitcast_fusion
  9.3 14.8 %convert_reduce_fusion = (f32[8,128]{1,0:T(8,128)S(1)}, bf16[8,32,128,128]{3,1,2,0:T(8,128)(2,1)}) fusion(bf16[128,128,128]{2,1,0:T(8,128)(2,1)} %bitcast.70, s32[8,32]{1,0:T(8,128)S(1)} %multiply_add_fusion, s32[128]{0:T(128)S(1)} %add_bitcast_fusion, pred[128]{0:T(512)(128)(4,1)S(1)} %iota_compare_fusion), kind=kOutput, calls=%fused_computation | convolution fusion | flops 1086389248 | bytes 12588672 | tf_op jit(solution)/shard_map/kab,kij->aibj/dot_general | solution.py:22
  24.1 10.6 %all_to_all.36 = f32[8,1,1024]{2,1,0:T(1,128)S(1)} all-to-all(f32[8,1,1024]{2,1,0:T(1,128)S(1)} %broadcast_in_dim.17), channel_id=1, replica_groups=mesh['row'=32,'col'=8] {'col'}, dimensions={0} | all-to-all | bytes 65536 | tf_op jit(solution)/shard_map/all_to_all | solution.py:28
  34.7 1.1 broadcast_in_dim.19
  35.7 4.8 %all-to-all-start.1 = ((bf16[8,128,512]{2,1,0:T(8,128)(2,1)}), bf16[8,128,512]{2,1,0:T(8,128)(2,1)S(1)}, u32[]{:S(2)}, u32[]{:S(2)}) async-start(bf16[8,128,512]{2,1,0:T(8,128)(2,1)} %broadcast_in_dim.19), calls=%async_computation.1 | async-start | bytes 2097152 | tf_op jit(solution)/shard_map/all_to_all | solution.py:35
  40.6 13.4 %all-to-all-done.1 = bf16[8,128,512]{2,1,0:T(8,128)(2,1)S(1)} async-done(((bf16[8,128,512]{2,1,0:T(8,128)(2,1)}), bf16[8,128,512]{2,1,0:T(8,128)(2,1)S(1)}, u32[]{:S(2)}, u32[]{:S(2)}) %all-to-all-start.1) | async-done | bytes 1048608 | tf_op jit(solution)/shard_map/all_to_all | solution.py:35
  54.0 10.4 %fusion.5 = bf16[4096,512]{1,0:T(8,128)(2,1)} fusion(bf16[128,8,32,128]{3,2,1,0:T(8,128)(2,1)} %bitcast.63, bf16[1024,512]{1,0:T(8,128)(2,1)S(1)} %bitcast.66, bf16[512,512]{1,0:T(8,128)(2,1)S(1)} %copy-done, f32[1024]{0:T(1024)S(1)} %get-tuple-element.8), kind=kOutput, calls=%fused_computation.7 | convolution fusion | flops 4834983936 | bytes 14159872 | tf_op jit(solution)/shard_map/dot_general | solution.py:41
  64.4 10.5 %all-to-all-start.2 = ((bf16[32,128,512]{2,1,0:T(8,128)(2,1)}), bf16[32,128,512]{2,1,0:T(8,128)(2,1)}, u32[]{:S(2)}, u32[]{:S(2)}) async-start(bf16[32,128,512]{2,1,0:T(8,128)(2,1)} %bitcast.68), calls=%async_computation.3 | async-start | bytes 8388608 | tf_op jit(solution)/shard_map/all_to_all | solution.py:45
  75.0 0.2 reduce-scatter.2.cloned.1.call-start
  75.2 44.4 %all-gather.2.cloned.1.call-done = bf16[1,32,128,512]{3,2,0,1:T(8,128)(2,1)} async-done(((bf16[1,1,128,512]{3,2,0,1:T(8,128)(2,1)}), bf16[1,32,128,512]{3,2,0,1:T(8,128)(2,1)}) %all-gather.2.cloned.1.call-update) | async-done | bytes 4194320 | tf_op jit(solution)/shard_map/all_gather | solution.py:51
  119.6 9.3 %fusion.3 = f32[8,128,512,1]{2,1,3,0:T(8,128)} fusion(bf16[8,128,32,128]{3,2,1,0:T(8,128)(2,1)} %bitcast.64, bf16[32,128,512]{2,1,0:T(8,128)(2,1)} %bitcast.75), kind=kOutput, calls=%fused_computation.4 | convolution fusion | flops 4294967296 | bytes 14680064 | tf_op jit(solution)/shard_map/aibj,bjf->aif/dot_general | solution.py:53
  128.9 2.4 convolution_bitcast_fusion
  131.3 47.4 %all-to-all-done.2 = bf16[32,128,512]{2,1,0:T(8,128)(2,1)} async-done(((bf16[32,128,512]{2,1,0:T(8,128)(2,1)}), bf16[32,128,512]{2,1,0:T(8,128)(2,1)}, u32[]{:S(2)}, u32[]{:S(2)}) %all-to-all-start.2) | async-done | bytes 4194336 | tf_op jit(solution)/shard_map/all_to_all | solution.py:45
  178.7 29.8 %all_to_all.37 = f32[8,64,512]{2,1,0:T(8,128)S(1)} all-to-all(f32[8,64,512]{2,1,0:T(8,128)S(1)} %bitcast.67), channel_id=1, replica_groups=mesh['row'=32,'col'=8] {'col'}, dimensions={0} | all-to-all | bytes 2097152 | tf_op jit(solution)/shard_map/all_to_all | solution.py:65
  208.6 17.2 %all_to_all.38 = f32[32,2,512]{2,1,0:T(2,128)S(1)} all-to-all(f32[32,2,512]{2,1,0:T(2,128)S(1)} %reshape.112), channel_id=1, replica_groups=mesh['row'=32,'col'=8] {'row'}, dimensions={0} | all-to-all | bytes 262144 | tf_op jit(solution)/shard_map/all_to_all | solution.py:67
  225.9 14.9 %all_to_all.39 = f32[32,2,512]{2,1,0:T(2,128)S(1)} all-to-all(f32[32,2,512]{2,1,0:T(2,128)S(1)} %broadcast_in_dim.40), channel_id=1, replica_groups=mesh['row'=32,'col'=8] {'row'}, dimensions={0} | all-to-all | bytes 262144 | tf_op jit(solution)/shard_map/all_to_all | solution.py:69
  240.9 1.1 broadcast_in_dim.42
  242.0 6.3 %all-to-all-start.6 = ((f32[8,64,512]{2,1,0:T(8,128)}), f32[8,64,512]{2,1,0:T(8,128)S(1)}, u32[]{:S(2)}, u32[]{:S(2)}) async-start(f32[8,64,512]{2,1,0:T(8,128)} %broadcast_in_dim.42), calls=%async_computation.7 | async-start | bytes 2097152 | tf_op jit(solution)/shard_map/all_to_all | solution.py:71
  248.3 4.6 %fusion.10 = bf16[1,128,512]{2,0,1:T(2,128)(2,1)S(1)} fusion(bf16[32,128,512]{2,1,0:T(8,128)(2,1)} %all-to-all-done.2), kind=kOutput, calls=%fused_computation.10 | convolution fusion | flops 4194304 | bytes 4325376 | tf_op jit(solution)/shard_map/r,rnf->nf/dot_general | solution.py:47
  253.0 0.7 copy.59
  253.7 8.5 %all-to-all-done.6 = f32[8,64,512]{2,1,0:T(8,128)S(1)} async-done(((f32[8,64,512]{2,1,0:T(8,128)}), f32[8,64,512]{2,1,0:T(8,128)S(1)}, u32[]{:S(2)}, u32[]{:S(2)}) %all-to-all-start.6) | async-done | bytes 1048608 | tf_op jit(solution)/shard_map/all_to_all | solution.py:71
  262.1 1.9 fusion.14
  264.0 1.0 copy.62
  (19 shorter events, 0.6 us)
Async XLA Ops:
  7.2 46.8 %copy-start = (bf16[512,512]{1,0:T(8,128)(2,1)S(1)}, bf16[512,512]{1,0:T(8,128)(2,1)}, u32[]{:S(2)}) copy-start(bf16[512,512]{1,0:T(8,128)(2,1)} %param.8) | copy-start | bytes 1572868
  7.2 112.4 %all-gather.2.cloned.1.call-start = ((), (), s32[]{:S(2)}) async-start(), calls=%async_computation.8 | async-start | bytes 4325376 | tf_op jit(solution)/shard_map/all_gather | solution.py:51
  9.3 25.4 %copy-start.1 = (bf16[1,1,128,512]{3,2,1,0:T(8,128)(2,1)S(1)}, bf16[1,1,128,512]{3,2,1,0:T(8,128)(2,1)}, u32[]{:S(2)}) copy-start(bf16[1,1,128,512]{3,2,1,0:T(8,128)(2,1)} %param.9) | copy-start | bytes 393220
  35.7 18.2 %all-to-all-start.1 = ((bf16[8,128,512]{2,1,0:T(8,128)(2,1)}), bf16[8,128,512]{2,1,0:T(8,128)(2,1)S(1)}, u32[]{:S(2)}, u32[]{:S(2)}) async-start(bf16[8,128,512]{2,1,0:T(8,128)(2,1)} %broadcast_in_dim.19), calls=%async_computation.1 | async-start | bytes 2097152 | tf_op jit(solution)/shard_map/all_to_all | solution.py:35
  64.4 114.3 %all-to-all-start.2 = ((bf16[32,128,512]{2,1,0:T(8,128)(2,1)}), bf16[32,128,512]{2,1,0:T(8,128)(2,1)}, u32[]{:S(2)}, u32[]{:S(2)}) async-start(bf16[32,128,512]{2,1,0:T(8,128)(2,1)} %bitcast.68), calls=%async_computation.3 | async-start | bytes 8388608 | tf_op jit(solution)/shard_map/all_to_all | solution.py:45
  75.0 187.1 %reduce-scatter.2.cloned.1.call-start = ((), (), s32[]{:S(2)}) async-start(), calls=%async_computation.9 | async-start | bytes 2359296 | tf_op jit(solution)/shard_map/reduce_scatter | solution.py:60
  242.0 20.1 %all-to-all-start.6 = ((f32[8,64,512]{2,1,0:T(8,128)}), f32[8,64,512]{2,1,0:T(8,128)S(1)}, u32[]{:S(2)}, u32[]{:S(2)}) async-start(f32[8,64,512]{2,1,0:T(8,128)} %broadcast_in_dim.42), calls=%async_computation.7 | async-start | bytes 2097152 | tf_op jit(solution)/shard_map/all_to_all | solution.py:71
Sparse Core Ops, SparseCore 0:
  10.8 108.7 all-gather.1
  129.0 79.4 reduce-scatter.1

commit v6 on v5

--- a/solution.py
+++ b/solution.py
@@ -41,12 +41,21 @@
     back_t = lax.dot_general(
         scaled, dense_flat, (((0,), (0,)), ((), ())), preferred_element_type=jnp.float32
     )
-    pieces = back_t.astype(jnp.bfloat16).T.reshape(rows_axis, sub_rows, width)
+    half = width // 2
+    odd = lax.axis_index("row") % 2 == 1
+    low, high = back_t[:half], back_t[half:]
+    keep = jnp.where(odd, high, low)
+    give = jnp.where(odd, low, high)
+    partner = [(i, i ^ 1) for i in range(rows_axis)]
+    chip_sum = keep + lax.ppermute(give, "row", partner)
+    pieces = chip_sum.astype(jnp.bfloat16).T.reshape(rows_axis, sub_rows, half)
     arrived = lax.all_to_all(pieces, "row", 0, 0)
-    ones = jnp.ones((rows_axis,), jnp.bfloat16)
-    feature_grad = jnp.einsum(
-        "r,rnf->nf", ones, arrived, preferred_element_type=jnp.float32
-    ).astype(jnp.bfloat16)
+    parity = jnp.arange(rows_axis, dtype=jnp.int32) % 2
+    from_even = (parity == 0).astype(jnp.bfloat16)
+    from_odd = (parity == 1).astype(jnp.bfloat16)
+    grad_low = jnp.einsum("r,rnf->nf", from_even, arrived, preferred_element_type=jnp.float32)
+    grad_high = jnp.einsum("r,rnf->nf", from_odd, arrived, preferred_element_type=jnp.float32)
+    feature_grad = jnp.concatenate([grad_low, grad_high], axis=1).astype(jnp.bfloat16)
 
     panel = lax.all_gather(features, "row", axis=1, tiled=True).reshape(tile_cols_blk, tile, width)
     panel, _ = lax.optimization_barrier((panel, pieces))

time: 272 us -> 260 us (0.956)
  waiting for transfers between devices: 114 us -> 91.9 us
  other arithmetic: 0.87 us -> 8.89 us
  local copies, waits for them, and re-layouts: 4.11 us -> 8.15 us
    all_to_all x1, waiting for transfers between devices: 47.4 us -> 0.01 us  [per_device(): arrived = lax.all_to_all(pieces, 'row', 0, 0)]
    all_gather x1, waiting for transfers between devices: 44.4 us -> 62.4 us  [per_device(): lax.all_gather(features, 'row', axis=1, tiled=True)]
    ppermute x0 -> x1, waiting for transfers between devices: none -> 7.15 us  [per_device(): chip_sum = keep + lax.ppermute(give, 'row', partner)]
    select_n x0 -> x1, other arithmetic: none -> 4.11 us  [per_device(): give = jnp.where(odd, low, high)]
    dot_general x1 -> x2, matrix products: 4.63 us -> 0.78 us  [the longest x1 0.39 us: per_device(): jnp.einsum('r,rnf->nf', from_odd, arrived, preferred_element_type=jnp.flo...]
    all_to_all x0 -> x1, local copies, waits for them, and re-layouts: none -> 3.4 us  [per_device(): arrived = lax.all_to_all(pieces, 'row', 0, 0)]
  transfers between devices with their start and end apart: 5 -> 6, of which waited for: 4 -> 4; matrix products, arithmetic and copies ran while one was open for 17% -> 14% of each run, Pallas kernels for 0% -> 0%
where the time goes in v6:
time: 260 us; the launch traced here: 259 us
  waiting for transfers between devices  91.9 us (35%)
  blocking collectives  72.1 us (28%)
  matrix products  41 us (16%)
  starting transfers between devices  22.2 us (9%)
  between operations  14.9 us (6%)
  other arithmetic  8.89 us (3%)
  local copies, waits for them, and re-layouts  8.15 us (3%)
    all_gather x1, waiting for transfers between devices, per_device(): lax.all_gather(features, 'row', axis=1, tiled=True)  62.4 us
    all_to_all x1, blocking collectives, per_device(): weight_part = jnp.sum(lax.all_to_all(weight_pieces, 'col', 0, 0), axis=0)  30.5 us
    all_to_all x1, blocking collectives, per_device(): lax.all_to_all(weight_pieces, 'row', 0, 0)  16.1 us
    all_to_all x1, blocking collectives, per_device(): lax.all_to_all(spread, 'row', 0, 0).reshape(width // cols_axis, width)  14.9 us
    dot_general x1, matrix products, per_device(): jnp.einsum('kab,kij->aibj', onehot, tile_vals[0, 0], preferred_element_ty...  14.8 us
    all_to_all x1, waiting for transfers between devices, per_device(): lax.all_to_all(grad_spread, 'col', 0, 0)  12.6 us
    all_to_all x1, blocking collectives, per_device(): deg_all = jnp.sum(lax.all_to_all(deg_spread, 'col', 0, 0), axis=0)  10.6 us
    dot_general x1, matrix products, per_device(): lax.dot_general(scaled, dense_flat, (((0,), (0,)), ((), ())), preferred_e...  10.6 us
  transfers between devices with their start and end apart: 6, of which 4 were waited for; matrix products, arithmetic and copies ran while one was open for 14% of the time, Pallas kernels for 0%

profile of v6, /device:TPU:2, one launch (start us, length us, event | category | flops | bytes accessed | tf_op | source)
XLA Modules:
  0.0 259.2 jit_solution(1256809355064156833)
XLA Ops:
  8.6 14.8 %convert_reduce_fusion = (f32[8,128]{1,0:T(8,128)S(1)}, bf16[8,32,128,128]{3,1,2,0:T(8,128)(2,1)}) fusion(bf16[128,128,128]{2,1,0:T(8,128)(2,1)} %bitcast.87, s32[8,32]{1,0:T(8,128)S(1)} %multiply_add_fusion, s32[128]{0:T(128)S(1)} %add_bitcast_fusion, pred[128]{0:T(512)(128)(4,1)S(1)} %iota_compare_fusion), kind=kOutput, calls=%fused_computation | convolution fusion | flops 1086389248 | bytes 12588672 | tf_op jit(solution)/shard_map/kab,kij->aibj/dot_general | solution.py:22
  23.4 10.6 %all_to_all.36 = f32[8,1,1024]{2,1,0:T(1,128)S(1)} all-to-all(f32[8,1,1024]{2,1,0:T(1,128)S(1)} %broadcast_in_dim.15), channel_id=1, replica_groups=mesh['row'=32,'col'=8] {'col'}, dimensions={0} | all-to-all | bytes 65536 | tf_op jit(solution)/shard_map/all_to_all | solution.py:28
  34.0 1.1 broadcast_in_dim.17
  35.1 4.8 %all-to-all-start.1 = ((bf16[8,128,512]{2,1,0:T(8,128)(2,1)}), bf16[8,128,512]{2,1,0:T(8,128)(2,1)S(1)}, u32[]{:S(2)}, u32[]{:S(2)}) async-start(bf16[8,128,512]{2,1,0:T(8,128)(2,1)} %broadcast_in_dim.17), calls=%async_computation.1 | async-start | bytes 2097152 | tf_op jit(solution)/shard_map/all_to_all | solution.py:35
  39.9 0.7 all-gather.2.cloned.1.call-update
  40.7 12.6 %all-to-all-done.1 = bf16[8,128,512]{2,1,0:T(8,128)(2,1)S(1)} async-done(((bf16[8,128,512]{2,1,0:T(8,128)(2,1)}), bf16[8,128,512]{2,1,0:T(8,128)(2,1)S(1)}, u32[]{:S(2)}, u32[]{:S(2)}) %all-to-all-start.1) | async-done | bytes 1048608 | tf_op jit(solution)/shard_map/all_to_all | solution.py:35
  53.3 10.6 %fusion = f32[512,4096]{1,0:T(8,128)} fusion(bf16[128,8,32,128]{3,2,1,0:T(8,128)(2,1)} %bitcast.82, bf16[1024,512]{1,0:T(8,128)(2,1)S(1)} %bitcast.85, bf16[512,512]{1,0:T(8,128)(2,1)S(1)} %copy-done, f32[1024]{0:T(1024)S(1)} %get-tuple-element.8), kind=kOutput, calls=%fused_computation.1 | convolution fusion | flops 4832886784 | bytes 18354176 | tf_op jit(solution)/shard_map/dot_general | solution.py:41
  63.9 4.1 %slice_select_fusion = f32[256,4096]{1,0:T(8,128)S(1)} fusion(f32[512,4096]{1,0:T(8,128)} %fusion, pred[]{:T(512)S(6)} %eq.45), kind=kLoop, calls=%fused_computation.11 | loop fusion | flops 1048576 | bytes 12582913 | tf_op jit(solution)/shard_map/jit(_where)/select_n | solution.py:48
  68.1 7.1 %collective-permute-done = f32[256,4096]{1,0:T(8,128)S(1)} collective-permute-done((f32[256,4096]{1,0:T(8,128)S(1)}, f32[256,4096]{1,0:T(8,128)S(1)}, u32[]{:S(2)}, u32[]{:S(2)}) %collective-permute-start) | collective-permute-done | bytes 4194336 | tf_op jit(solution)/shard_map/ppermute | solution.py:50
  75.3 2.0 copy_bitcast_fusion
  77.3 10.4 %all-to-all-start.2 = ((bf16[32,128,256]{1,2,0:T(8,128)(2,1)}), bf16[32,128,256]{1,2,0:T(8,128)(2,1)S(1)}, u32[]{:S(2)}, u32[]{:S(2)}) async-start(bf16[32,128,256]{1,2,0:T(8,128)(2,1)} %copy_bitcast_fusion), calls=%async_computation.3 | async-start | bytes 4194304 | tf_op jit(solution)/shard_map/all_to_all | solution.py:52
  87.9 62.4 %all-gather.2.cloned.1.call-done = bf16[1,32,128,512]{3,2,0,1:T(8,128)(2,1)} async-done(((bf16[1,1,128,512]{3,2,0,1:T(8,128)(2,1)}), bf16[1,32,128,512]{3,2,0,1:T(8,128)(2,1)}) %all-gather.2.cloned.1.call-update) | async-done | bytes 4194320 | tf_op jit(solution)/shard_map/all_gather | solution.py:60
  150.3 9.3 %fusion.3 = f32[8,128,512,1]{2,1,3,0:T(8,128)} fusion(bf16[8,128,32,128]{3,2,1,0:T(8,128)(2,1)} %bitcast.83, bf16[32,128,512]{2,1,0:T(8,128)(2,1)} %bitcast.91), kind=kOutput, calls=%fused_computation.4 | convolution fusion | flops 4294967296 | bytes 14680064 | tf_op jit(solution)/shard_map/aibj,bjf->aif/dot_general | solution.py:62
  159.7 3.7 %convolution_bitcast_fusion = f32[512,512]{1,0:T(8,128)} fusion(bf16[8,128,512]{2,1,0:T(8,128)(2,1)} %copy-done.3, f32[8,128,512,1]{2,1,3,0:T(8,128)} %fusion.3, f32[8,128]{1,0:T(8,128)S(1)} %get-tuple-element.7), kind=kOutput, calls=%fused_computation.16 | convolution fusion | flops 537919488 | bytes 4198400 | tf_op jit(solution)/shard_map/dot_general | solution.py:65
  163.4 30.5 %all_to_all.37 = f32[8,64,512]{2,1,0:T(8,128)} all-to-all(f32[8,64,512]{2,1,0:T(8,128)} %bitcast.86), channel_id=1, replica_groups=mesh['row'=32,'col'=8] {'col'}, dimensions={0} | all-to-all | bytes 2097152 | tf_op jit(solution)/shard_map/all_to_all | solution.py:74
  193.9 1.3 reduce_sum.38
  195.3 16.1 %all_to_all.38 = f32[32,2,512]{2,1,0:T(2,128)S(1)} all-to-all(f32[32,2,512]{2,1,0:T(2,128)S(1)} %reshape.141), channel_id=1, replica_groups=mesh['row'=32,'col'=8] {'row'}, dimensions={0} | all-to-all | bytes 262144 | tf_op jit(solution)/shard_map/all_to_all | solution.py:76
  211.5 14.9 %all_to_all.39 = f32[32,2,512]{2,1,0:T(2,128)S(1)} all-to-all(f32[32,2,512]{2,1,0:T(2,128)S(1)} %broadcast_in_dim.18), channel_id=1, replica_groups=mesh['row'=32,'col'=8] {'row'}, dimensions={0} | all-to-all | bytes 262144 | tf_op jit(solution)/shard_map/all_to_all | solution.py:78
  226.5 1.1 broadcast_in_dim.39
  227.6 6.7 %all-to-all-start.6 = ((f32[8,64,512]{2,1,0:T(8,128)}), f32[8,64,512]{2,1,0:T(8,128)}, u32[]{:S(2)}, u32[]{:S(2)}) async-start(f32[8,64,512]{2,1,0:T(8,128)} %broadcast_in_dim.39), calls=%async_computation.7 | async-start | bytes 2097152 | tf_op jit(solution)/shard_map/all_to_all | solution.py:80
  234.4 3.4 %copy.39 = bf16[32,128,256]{2,0,1:T(8,128)(2,1)S(1)} copy(bf16[32,128,256]{1,2,0:T(8,128)(2,1)} %copy-done.2) | data formatting | bytes 4194304 | tf_op jit(solution)/shard_map/all_to_all | solution.py:52
  239.2 9.0 %all-to-all-done.6 = f32[8,64,512]{2,1,0:T(8,128)} async-done(((f32[8,64,512]{2,1,0:T(8,128)}), f32[8,64,512]{2,1,0:T(8,128)}, u32[]{:S(2)}, u32[]{:S(2)}) %all-to-all-start.6) | async-done | bytes 1048608 | tf_op jit(solution)/shard_map/all_to_all | solution.py:80
  248.2 1.9 fusion.9
  250.1 2.3 copy.68
  (32 shorter events, 2.9 us)
Async XLA Ops:
  7.2 46.2 %copy-start = (bf16[512,512]{1,0:T(8,128)(2,1)S(1)}, bf16[512,512]{1,0:T(8,128)(2,1)}, u32[]{:S(2)}) copy-start(bf16[512,512]{1,0:T(8,128)(2,1)} %param.8) | copy-start | bytes 1572868
  8.6 25.4 %copy-start.4 = (bf16[1,1,128,512]{3,2,1,0:T(8,128)(2,1)S(1)}, bf16[1,1,128,512]{3,2,1,0:T(8,128)(2,1)}, u32[]{:S(2)}) copy-start(bf16[1,1,128,512]{3,2,1,0:T(8,128)(2,1)} %param.9) | copy-start | bytes 393220
  35.1 18.2 %all-to-all-start.1 = ((bf16[8,128,512]{2,1,0:T(8,128)(2,1)}), bf16[8,128,512]{2,1,0:T(8,128)(2,1)S(1)}, u32[]{:S(2)}, u32[]{:S(2)}) async-start(bf16[8,128,512]{2,1,0:T(8,128)(2,1)} %broadcast_in_dim.17), calls=%async_computation.1 | async-start | bytes 2097152 | tf_op jit(solution)/shard_map/all_to_all | solution.py:35
  39.9 110.4 %all-gather.2.cloned.1.call-start = ((), (), s32[]{:S(2)}) async-start(), calls=%async_computation.8 | async-start | bytes 4325376 | tf_op jit(solution)/shard_map/all_gather | solution.py:60
  53.3 10.6 %copy-start.3 = (bf16[8,128,512]{2,1,0:T(8,128)(2,1)}, bf16[8,128,512]{2,1,0:T(8,128)(2,1)S(1)}, u32[]{:S(2)}) copy-start(bf16[8,128,512]{2,1,0:T(8,128)(2,1)S(1)} %all-to-all-done.1) | copy-start | bytes 3145732
  63.9 11.4 %copy-start.1 = (f32[512,4096]{1,0:T(8,128)S(1)}, f32[512,4096]{1,0:T(8,128)}, u32[]{:S(2)}) copy-start(f32[512,4096]{1,0:T(8,128)} %fusion) | copy-start | bytes 25165828
  68.0 7.2 %collective-permute-start = (f32[256,4096]{1,0:T(8,128)S(1)}, f32[256,4096]{1,0:T(8,128)S(1)}, u32[]{:S(2)}, u32[]{:S(2)}) collective-permute-start(f32[256,4096]{1,0:T(8,128)S(1)} %slice_select_fusion), channel_id=1, source_target_pairs={{0,8},{8,0},{16,24},{24,16},{32,40},{40,32},{48,56},{56,48},{64,72... | collective-permute-start | bytes 12582920 | tf_op jit(solution)/shard_map/ppermute | solution.py:50
  77.3 86.1 %all-to-all-start.2 = ((bf16[32,128,256]{1,2,0:T(8,128)(2,1)}), bf16[32,128,256]{1,2,0:T(8,128)(2,1)S(1)}, u32[]{:S(2)}, u32[]{:S(2)}) async-start(bf16[32,128,256]{1,2,0:T(8,128)(2,1)} %copy_bitcast_fusion), calls=%async_computation.3 | async-start | bytes 4194304 | tf_op jit(solution)/shard_map/all_to_all | solution.py:52
  87.7 160.5 %reduce-scatter.2.cloned.1.call-start = ((), (), s32[]{:S(2)}) async-start(), calls=%async_computation.9 | async-start | bytes 2359296 | tf_op jit(solution)/shard_map/reduce_scatter | solution.py:69
  163.4 70.9 %copy-start.2 = (bf16[32,128,256]{1,2,0:T(8,128)(2,1)}, bf16[32,128,256]{1,2,0:T(8,128)(2,1)S(1)}, u32[]{:S(2)}) copy-start(bf16[32,128,256]{1,2,0:T(8,128)(2,1)S(1)} %all-to-all-done.2) | copy-start | bytes 6291460
  227.6 20.6 %all-to-all-start.6 = ((f32[8,64,512]{2,1,0:T(8,128)}), f32[8,64,512]{2,1,0:T(8,128)}, u32[]{:S(2)}, u32[]{:S(2)}) async-start(f32[8,64,512]{2,1,0:T(8,128)} %broadcast_in_dim.39), calls=%async_computation.7 | async-start | bytes 2097152 | tf_op jit(solution)/shard_map/all_to_all | solution.py:80
Sparse Core Ops, SparseCore 0:
  43.5 106.8 all-gather.1
  159.8 63.7 reduce-scatter.1
